TPU v7x, 1024 devices: a whole 8x8x8 slice. The times are simulated.
1024 devices in a mesh: gx: 32 (over x, z_hi, core), gy: 32 (over y, z_lo).
Axes of the slice: x: 8, y: 8, z: 8 (z_hi: 2, z_lo: 4; z = z_hi * 4 + z_lo), core: 2. Of those that a mesh axis runs over, the one named last changes fastest.
Arguments:
- flow_state: float32 [20, 128, 192, 128], P(None, 'gx', 'gy'), may hold values from -6 to 6
- reacting: int32 [128, 192], P('gx', 'gy'), may hold values from 0 to 1, as said below
- w_in: bfloat16 [20, 1600], replicated, may hold values from -1.25 to 1.25
- w_mid: bfloat16 [1600, 800], replicated, may hold values from -0.15625 to 0.15625
- w_low: bfloat16 [800, 400], replicated, may hold values from -0.21875 to 0.21875
- w_out: bfloat16 [20, 400], replicated, may hold values from -0.3125 to 0.3125
- diffusivity: float32 [20], replicated, may hold values from 0.1 to 1
Outputs:
- new_state: float32 [20, 128, 192, 128], P(None, 'gx', 'gy')
Inputs may be any that keep to these rules, and one draw needn't show every extreme that they name: Tiles are the 4 x 6 blocks of columns whose first indices start at multiples of 4 and 6. In every band of 6 columns along the second dimension that starts at a multiple of 6, exactly 288 columns react; every tile holds between 0 and 18 reacting columns, its count differing from 9 by at least 5, and in every band some tile holds 18 and some tile 0. In the first band, the first 16 tiles along the first dimension hold 18 each and the others 0 each.
All inputs are finite; a program needn't handle non-finite values.
Results may differ from a plain program's by a relative error of at most 0.00055.
Values may be sent and summed in bfloat16 or wider, within the bound.
No kernel may reach another device: no remote copies, remote signals or barrier semaphores. Data moves between devices by JAX's collectives and lax.ppermute only.
A program may use at most 32 MiB of HBM per device.

v0:
```python
import jax
import jax.numpy as jnp
from jax import lax
from jax.sharding import PartitionSpec as P

step_size = 0.05
reaction_gain = 8.0
velocity_x = 1.0
velocity_y = -0.6
velocity_z = 0.35


def padded_2(x, sides, width):
    for axis, dim in sides:
        peers, length = (lax.axis_size(axis), x.shape[dim])
        up = [(i, (i + 1) % peers) for i in range(peers)]
        down = [(j, i) for i, j in up]
        last = lax.slice_in_dim(x, length - width, length, axis=dim)
        leading = lax.slice_in_dim(x, 0, width, axis=dim)
        before = lax.ppermute(last, axis, up)
        after = lax.ppermute(leading, axis, down)
        x = jnp.concatenate([before, x, after], axis=dim)
    return x


def stencil(shifted):
    plus_one = shifted(1)
    plus_two = shifted(2)
    minus_one = shifted(-1)
    minus_two = shifted(-2)
    slope = (8.0 * (plus_one - minus_one) - (plus_two - minus_two)) / 12.0
    curve = (16.0 * (plus_one + minus_one) - (plus_two + minus_two) - 30.0 * shifted(0)) / 12.0
    return (slope, curve)


def transport(field_set, diffusivity):
    wide_x = field_set.shape[1]
    wide_y = field_set.shape[2]
    padded = padded_2(field_set.astype(jnp.bfloat16), (("gx", 1), ("gy", 2)), 2).astype(
        field_set.dtype
    )
    slope_x, curve_x = stencil(
        lambda step_k: padded[:, 2 + step_k : 2 + step_k + wide_x, 2 : 2 + wide_y, :]
    )
    slope_y, curve_y = stencil(
        lambda step_k: padded[:, 2 : 2 + wide_x, 2 + step_k : 2 + step_k + wide_y, :]
    )
    slope_z, curve_z = stencil(lambda step_k: jnp.roll(field_set, -step_k, axis=3))
    return -(velocity_x * slope_x + velocity_y * slope_y + velocity_z * slope_z) + diffusivity[
        :, None, None, None
    ] * (curve_x + curve_y + curve_z)


def network(cell_rows, w_in, w_mid, w_low, w_out):
    hidden = jax.nn.silu(
        jnp.einsum("bfz,fh->bzh", cell_rows, w_in, preferred_element_type=jnp.float32)
    ).astype(jnp.bfloat16)
    hidden = jax.nn.silu(
        jnp.einsum("bzh,hk->bzk", hidden, w_mid, preferred_element_type=jnp.float32)
    ).astype(jnp.bfloat16)
    hidden = jax.nn.silu(
        jnp.einsum("bzk,kj->bzj", hidden, w_low, preferred_element_type=jnp.float32)
    ).astype(jnp.bfloat16)
    return jnp.einsum("bzj,fj->bfz", hidden, w_out, preferred_element_type=jnp.float32).astype(
        jnp.bfloat16
    )


def body(flow_state, reacting, w_in, w_mid, w_low, w_out, diffusivity):
    fields, wide_x, wide_y, depth_z = flow_state.shape
    blocks = wide_x * wide_y
    groups = lax.axis_size("gx")
    share = 3 * blocks // 8
    spread = min(share, blocks - share)
    live_mask = reacting.reshape(blocks)
    live_count = jnp.sum(live_mask)
    local_rank = jnp.cumsum(live_mask) - live_mask
    extra = jnp.maximum(live_count - share, 0)
    short = jnp.maximum(share - live_count, 0)
    count_table = lax.all_gather(
        jnp.stack([live_count, extra, short]).reshape(1, 3), "gx", axis=0, tiled=True
    )
    below = (jnp.arange(groups) < lax.axis_index("gx")).astype(jnp.int32)
    offsets = jnp.sum(count_table * below[:, None], axis=0)
    extra_offset = offsets[1]
    short_offset = offsets[2]
    slots = jnp.arange(spread)
    keep_pick = (
        (local_rank[None, :] == jnp.arange(share)[:, None]) & (live_mask[None, :] == 1)
    ).astype(jnp.bfloat16)
    send_pick = (
        (local_rank[None, :] - share == slots[:, None]) & (live_mask[None, :] == 1)
    ).astype(jnp.bfloat16)
    kept_count = jnp.minimum(live_count, share)
    place = (
        (jnp.arange(share)[:, None] == kept_count + slots[None, :]) & (slots[None, :] < short)
    ).astype(jnp.bfloat16)
    extra_table = count_table[:, 1]
    short_table = count_table[:, 2]
    extra_starts = jnp.cumsum(extra_table) - extra_table
    short_starts = jnp.cumsum(short_table) - short_table

    def match_rows(count, start_table, limit_table, want_start, want_count):
        index = jnp.arange(count)
        sender = index // spread
        slot = index % spread
        sender_hot = (sender[:, None] == jnp.arange(groups)[None, :]).astype(jnp.int32)
        anchor = jnp.sum(sender_hot * start_table[None, :], axis=1)
        limit = jnp.sum(sender_hot * limit_table[None, :], axis=1)
        ident = jnp.where(slot < limit, anchor + slot, -1)
        return (
            (ident[None, :] == want_start + slots[:, None]) & (slots[:, None] < want_count)
        ).astype(jnp.bfloat16)

    rows = jnp.moveaxis(flow_state.reshape(fields, blocks, depth_z), 1, 0).astype(jnp.bfloat16)
    outgoing = jnp.einsum(
        "sb,bfz->sfz", send_pick, rows, preferred_element_type=jnp.float32
    ).astype(jnp.bfloat16)
    piece = lax.all_gather(outgoing, "gx", axis=0, tiled=True)
    matcher = match_rows(piece.shape[0], extra_starts, extra_table, short_offset, short)
    received = jnp.einsum("qs,sfz->qfz", matcher, piece, preferred_element_type=jnp.float32).astype(
        jnp.bfloat16
    )
    batch = jnp.einsum("qb,bfz->qfz", keep_pick, rows, preferred_element_type=jnp.float32)
    batch = (
        batch + jnp.einsum("qs,sfz->qfz", place, received, preferred_element_type=jnp.float32)
    ).astype(jnp.bfloat16)
    results = network(batch, w_in, w_mid, w_low, w_out)
    replies = jnp.einsum("qs,qfz->sfz", place, results, preferred_element_type=jnp.float32).astype(
        jnp.bfloat16
    )
    piece = lax.all_gather(replies, "gx", axis=0, tiled=True)
    matcher = match_rows(piece.shape[0], short_starts, short_table, extra_offset, extra)
    returned = jnp.einsum("qs,sfz->qfz", matcher, piece, preferred_element_type=jnp.float32).astype(
        jnp.bfloat16
    )
    source = jnp.einsum("qb,qfz->bfz", keep_pick, results, preferred_element_type=jnp.float32)
    source = source + jnp.einsum(
        "sb,sfz->bfz", send_pick, returned, preferred_element_type=jnp.float32
    )
    reaction = jnp.moveaxis(source, 0, 1).reshape(fields, wide_x, wide_y, depth_z)

    def tendency(field_set):
        return transport(field_set, diffusivity) + reaction_gain * reaction

    first_section = flow_state + step_size * tendency(flow_state)
    return 0.5 * flow_state + 0.5 * (first_section + step_size * tendency(first_section))


def solution(mesh):
    in_specs = (P(None, "gx", "gy", None), P("gx", "gy"), P(), P(), P(), P(), P())
    out_specs = P(None, "gx", "gy", None)
    return jax.shard_map(body, mesh=mesh, in_specs=in_specs, out_specs=out_specs, check_vma=False)
```

profile of v0, /device:TPU:1, one launch (start us, length us, event | category | flops | bytes accessed | tf_op | source)
XLA Modules:
  0.0 269.3 jit_solution(6539239706411529462)
XLA Ops:
  6.5 0.9 reshape.184
  7.5 0.8 reshape.204
  8.2 1.0 copy.114
  9.6 0.6 copy.66
  10.3 1.3 reduce_sum.54
  13.5 1.4 dynamic-slice
  15.6 0.8 add_dynamic-update-slice_fusion
  16.4 25.1 %all-reduce = s32[96]{0:T(128)S(1)} all-reduce(s32[96]{0:T(128)S(1)} %add_dynamic-update-slice_fusion), channel_id=2, replica_groups=mesh['gx'=32,'gy'=32] {'gx'}, use_global_device_ids=true, to_apply=%add | all-reduce | flops 96 | bytes 768
  42.3 0.6 fusion.114
  42.9 0.6 iota_add_fusion.1
  43.9 79.9 %all-gather.4.cloned.1.call-done = bf16[288,20,128]{2,1,0:T(8,128)(2,1)} async-done(((bf16[9,20,128]{2,1,0:T(8,128)(2,1)}), bf16[288,20,128]{2,1,0:T(8,128)(2,1)}) %all-gather.4.cloned.1.call-update) | async-done | bytes 1474576 | tf_op jit(solution)/shard_map/all_gather | solution.py:119
  123.8 2.0 fusion.11
  125.8 6.7 %fusion = f32[9,128,800]{1,2,0:T(8,128)} fusion(bf16[1600,800]{0,1:T(8,128)(2,1)S(1)} %copy-done, bf16[20,1600]{1,0:T(8,128)(2,1)S(1)} %copy-done.2, bf16[9,20,128]{2,0,1:T(8,128)(2,1)S(1)} %fusion.11), kind=kOutput, calls=%fused_computation.2 | convolution fusion | flops 3032064000 | bytes 6356480 | tf_op jit(solution)/shard_map/bzh,hk->bzk/dot_general | solution.py:59
  132.4 4.2 %fusion.22 = bf16[9,20,128]{2,1,0:T(8,128)(2,1)S(1)} fusion(f32[9,128,800]{1,2,0:T(8,128)} %fusion, bf16[800,400]{0,1:T(8,128)(2,1)} %param.11, bf16[20,400]{1,0:T(8,128)(2,1)S(1)} %copy-done.3), kind=kOutput, calls=%fused_computation.21 | convolution fusion | flops 762647040 | bytes 4388480 | tf_op jit(solution)/shard_map/bzj,fj->bfz/dot_general | solution.py:64
  136.7 0.2 convolution_convert_fusion
  136.9 0.6 copy.72
  137.6 1.9 collective-permute-start
  139.5 2.4 collective-permute-start.1
  141.9 0.2 fusion.110
  142.2 0.2 fusion.111
  142.4 0.8 copy.107
  143.1 0.8 copy.108
  143.9 0.8 copy.109
  144.7 0.2 fusion.108
  144.9 0.8 copy.110
  145.6 0.2 fusion.109
  145.8 0.8 copy.111
  146.6 0.8 copy.112
  147.3 0.8 copy.113
  148.2 1.5 collective-permute-done.1
  149.7 3.5 %collective-permute-start.2 = (bf16[20,8,2,128]{3,0,2,1:T(8,128)(2,1)S(1)}, bf16[20,8,2,128]{3,0,2,1:T(8,128)(2,1)S(1)}, u32[]{:S(2)}, u32[]{:S(2)}) collective-permute-start(bf16[20,8,2,128]{3,0,2,1:T(8,128)(2,1)S(1)} %get-tuple-element.25), channel_id=1, source_target_pairs={{0,1},{1,2},{2,3},{3,4},{4,5},{5,6},{6,7},{7,8},{8,9},{9,10},{10,1... | collective-permute-start | bytes 245768 | tf_op jit(solution)/shard_map/ppermute | solution.py:20
  153.2 5.6 %collective-permute-start.3 = (bf16[20,8,2,128]{3,0,2,1:T(8,128)(2,1)S(1)}, bf16[20,8,2,128]{3,0,2,1:T(8,128)(2,1)S(1)}, u32[]{:S(2)}, u32[]{:S(2)}) collective-permute-start(bf16[20,8,2,128]{3,0,2,1:T(8,128)(2,1)S(1)} %get-tuple-element.26), channel_id=1, source_target_pairs={{1,0},{2,1},{3,2},{4,3},{5,4},{6,5},{7,6},{8,7},{9,8},{10,9},{11,1... | collective-permute-start | bytes 245768 | tf_op jit(solution)/shard_map/ppermute | solution.py:21
  158.9 0.7 iota_add_fusion
  159.6 0.9 collective-permute-done.3
  160.5 1.1 maximum_convert_fusion
  161.6 0.9 fusion.37
  162.5 67.2 %all-gather.6.cloned.1.call-done = bf16[288,20,128]{2,1,0:T(8,128)(2,1)} async-done(((bf16[9,20,128]{2,1,0:T(8,128)(2,1)}), bf16[288,20,128]{2,1,0:T(8,128)(2,1)}) %all-gather.6.cloned.1.call-update) | async-done | bytes 1474576 | tf_op jit(solution)/shard_map/all_gather | solution.py:132
  229.7 2.7 %fusion.10 = f32[20,24,128]{2,1,0:T(8,128)} fusion(f32[24,20,128]{2,0,1:T(8,128)} %fusion.37, bf16[288,20,128]{2,1,0:T(8,128)(2,1)} %all-gather.6.cloned.1.call-done, s32[288]{0:T(512)S(1)} %add_select_fusion.2, s32[9]{0:T(128)S(1)} %iota_add_fusion, pred[9]{0:T(512)(128)(4,1)S(1)} %iota_compare_fusion.4, s32[24]{0:T(128)S(1)} %get-tuple-element.13, ...), kind=kOutput, calls=%fused_computation.13 | convolution fusion | flops 14528496 | bytes 1967397 | tf_op jit(solution)/shard_map/sb,sfz->bfz/dot_general | solution.py:138
  232.4 1.0 copy.74
  233.4 3.1 %fusion.102 = (bf16[20,4,6,128]{3,0,2,1:T(8,128)(2,1)S(1)}, f32[20,4,6,128]{3,0,2,1:T(8,128)S(1)}) fusion(f32[20,4,6,128]{3,0,2,1:T(8,128)S(1)} %bitcast.51, f32[20]{0:T(128)S(1)} %broadcast_multiply_fusion, f32[20,8,10,128]{3,0,2,1:T(8,128)} %maximum_convert_fusion, f32[20,4,6,126]{3,0,2,1:T(8,128)S(1)} %copy.106, f32[20,4,6,2]{3,0,2,1:T(8,128)} %copy.107, ...), kind=kLoop, calls=%fused_computation.128 | loop fusion | flops 2887680 | bytes 4055120 | tf_op jit(solution)/shard_map/convert_element_type | solution.py:39
  236.9 1.9 collective-permute-start.4
  238.8 2.4 collective-permute-start.5
  241.4 7.6 %collective-permute-done.5 = bf16[20,2,6,128]{3,0,2,1:T(8,128)(2,1)S(1)} collective-permute-done((bf16[20,2,6,128]{3,0,2,1:T(8,128)(2,1)S(1)}, bf16[20,2,6,128]{3,0,2,1:T(8,128)(2,1)S(1)}, u32[]{:S(2)}, u32[]{:S(2)}) %collective-permute-start.5) | collective-permute-done | bytes 61472 | tf_op jit(solution)/shard_map/ppermute | solution.py:21
  249.0 3.5 %collective-permute-start.6 = (bf16[20,8,2,128]{3,0,2,1:T(8,128)(2,1)S(1)}, bf16[20,8,2,128]{3,0,2,1:T(8,128)(2,1)S(1)}, u32[]{:S(2)}, u32[]{:S(2)}) collective-permute-start(bf16[20,8,2,128]{3,0,2,1:T(8,128)(2,1)S(1)} %get-tuple-element.23), channel_id=1, source_target_pairs={{0,1},{1,2},{2,3},{3,4},{4,5},{5,6},{6,7},{7,8},{8,9},{9,10},{10,1... | collective-permute-start | bytes 245768 | tf_op jit(solution)/shard_map/ppermute | solution.py:20
  252.6 5.6 %collective-permute-start.7 = (bf16[20,8,2,128]{3,0,2,1:T(8,128)(2,1)S(1)}, bf16[20,8,2,128]{3,0,2,1:T(8,128)(2,1)S(1)}, u32[]{:S(2)}, u32[]{:S(2)}) collective-permute-start(bf16[20,8,2,128]{3,0,2,1:T(8,128)(2,1)S(1)} %get-tuple-element.24), channel_id=1, source_target_pairs={{1,0},{2,1},{3,2},{4,3},{5,4},{6,5},{7,6},{8,7},{9,8},{10,9},{11,1... | collective-permute-start | bytes 245768 | tf_op jit(solution)/shard_map/ppermute | solution.py:21
  258.4 2.5 collective-permute-done.7
  261.0 0.6 fusion.29
  261.7 0.8 copy.77
  (53 shorter events, 2.3 us)
Async XLA Ops:
  6.5 119.2 %copy-start = (bf16[1600,800]{0,1:T(8,128)(2,1)S(1)}, bf16[1600,800]{0,1:T(8,128)(2,1)}, u32[]{:S(2)}) copy-start(bf16[1600,800]{0,1:T(8,128)(2,1)} %param.10) | copy-start | bytes 7680004
  6.5 119.2 %copy-start.2 = (bf16[20,1600]{1,0:T(8,128)(2,1)S(1)}, bf16[20,1600]{1,0:T(8,128)(2,1)}, u32[]{:S(2)}) copy-start(bf16[20,1600]{1,0:T(8,128)(2,1)} %param.9) | copy-start | bytes 192004
  6.5 117.2 %all-gather.4.cloned.1.call-start = ((), (), s32[]{:S(2)}) async-start(), calls=%async_computation | async-start | bytes 1824768 | tf_op jit(solution)/shard_map/all_gather | solution.py:119
  10.2 219.5 %all-gather.6.cloned.1.call-start = ((), (), s32[]{:S(2)}) async-start(), calls=%async_computation.1 | async-start | bytes 1824768 | tf_op jit(solution)/shard_map/all_gather | solution.py:132
  125.8 6.7 %copy-start.3 = (bf16[20,400]{1,0:T(8,128)(2,1)S(1)}, bf16[20,400]{1,0:T(8,128)(2,1)}, u32[]{:S(2)}) copy-start(bf16[20,400]{1,0:T(8,128)(2,1)} %param.12) | copy-start | bytes 48004
  132.4 9.5 %copy-start.1 = (f32[20,4,6,128]{3,1,2,0:T(4,128)S(1)}, f32[20,4,6,128]{3,1,2,0:T(4,128)}, u32[]{:S(2)}) copy-start(f32[20,4,6,128]{3,1,2,0:T(4,128)} %param.7) | copy-start | bytes 737284
  137.6 10.6 %collective-permute-start = (bf16[20,2,6,128]{3,0,2,1:T(8,128)(2,1)S(1)}, bf16[20,2,6,128]{3,0,2,1:T(8,128)(2,1)S(1)}, u32[]{:S(2)}, u32[]{:S(2)}) collective-permute-start(bf16[20,2,6,128]{3,0,2,1:T(8,128)(2,1)S(1)} %get-tuple-element.37), channel_id=1, source_target_pairs={{0,32},{32,64},{64,96},{96,128},{128,160},{160,192},{192,224},{224... | collective-permute-start | bytes 184328 | tf_op jit(solution)/shard_map/ppermute | solution.py:20
  139.5 10.1 %collective-permute-start.1 = (bf16[20,2,6,128]{3,0,2,1:T(8,128)(2,1)S(1)}, bf16[20,2,6,128]{3,0,2,1:T(8,128)(2,1)S(1)}, u32[]{:S(2)}, u32[]{:S(2)}) collective-permute-start(bf16[20,2,6,128]{3,0,2,1:T(8,128)(2,1)S(1)} %get-tuple-element.38), channel_id=1, source_target_pairs={{32,0},{64,32},{96,64},{128,96},{160,128},{192,160},{224,192},{256... | collective-permute-start | bytes 184328 | tf_op jit(solution)/shard_map/ppermute | solution.py:21
  143.1 5.0 %copy-start.4 = (f32[20]{0:T(128)S(1)}, f32[20]{0:T(128)}, u32[]{:S(2)}) copy-start(f32[20]{0:T(128)} %param.13) | copy-start | bytes 244
  149.7 9.9 %collective-permute-start.2 = (bf16[20,8,2,128]{3,0,2,1:T(8,128)(2,1)S(1)}, bf16[20,8,2,128]{3,0,2,1:T(8,128)(2,1)S(1)}, u32[]{:S(2)}, u32[]{:S(2)}) collective-permute-start(bf16[20,8,2,128]{3,0,2,1:T(8,128)(2,1)S(1)} %get-tuple-element.25), channel_id=1, source_target_pairs={{0,1},{1,2},{2,3},{3,4},{4,5},{5,6},{6,7},{7,8},{8,9},{9,10},{10,1... | collective-permute-start | bytes 245768 | tf_op jit(solution)/shard_map/ppermute | solution.py:20
  153.2 7.3 %collective-permute-start.3 = (bf16[20,8,2,128]{3,0,2,1:T(8,128)(2,1)S(1)}, bf16[20,8,2,128]{3,0,2,1:T(8,128)(2,1)S(1)}, u32[]{:S(2)}, u32[]{:S(2)}) collective-permute-start(bf16[20,8,2,128]{3,0,2,1:T(8,128)(2,1)S(1)} %get-tuple-element.26), channel_id=1, source_target_pairs={{1,0},{2,1},{3,2},{4,3},{5,4},{6,5},{7,6},{8,7},{9,8},{10,9},{11,1... | collective-permute-start | bytes 245768 | tf_op jit(solution)/shard_map/ppermute | solution.py:21
  236.9 4.5 %collective-permute-start.4 = (bf16[20,2,6,128]{3,0,2,1:T(8,128)(2,1)S(1)}, bf16[20,2,6,128]{3,0,2,1:T(8,128)(2,1)S(1)}, u32[]{:S(2)}, u32[]{:S(2)}) collective-permute-start(bf16[20,2,6,128]{3,0,2,1:T(8,128)(2,1)S(1)} %get-tuple-element.35), channel_id=1, source_target_pairs={{0,32},{32,64},{64,96},{96,128},{128,160},{160,192},{192,224},{224... | collective-permute-start | bytes 184328 | tf_op jit(solution)/shard_map/ppermute | solution.py:20
  238.8 10.2 %collective-permute-start.5 = (bf16[20,2,6,128]{3,0,2,1:T(8,128)(2,1)S(1)}, bf16[20,2,6,128]{3,0,2,1:T(8,128)(2,1)S(1)}, u32[]{:S(2)}, u32[]{:S(2)}) collective-permute-start(bf16[20,2,6,128]{3,0,2,1:T(8,128)(2,1)S(1)} %get-tuple-element.36), channel_id=1, source_target_pairs={{32,0},{64,32},{96,64},{128,96},{160,128},{192,160},{224,192},{256... | collective-permute-start | bytes 184328 | tf_op jit(solution)/shard_map/ppermute | solution.py:21
  249.0 9.4 %collective-permute-start.6 = (bf16[20,8,2,128]{3,0,2,1:T(8,128)(2,1)S(1)}, bf16[20,8,2,128]{3,0,2,1:T(8,128)(2,1)S(1)}, u32[]{:S(2)}, u32[]{:S(2)}) collective-permute-start(bf16[20,8,2,128]{3,0,2,1:T(8,128)(2,1)S(1)} %get-tuple-element.23), channel_id=1, source_target_pairs={{0,1},{1,2},{2,3},{3,4},{4,5},{5,6},{6,7},{7,8},{8,9},{9,10},{10,1... | collective-permute-start | bytes 245768 | tf_op jit(solution)/shard_map/ppermute | solution.py:20
  252.6 8.4 %collective-permute-start.7 = (bf16[20,8,2,128]{3,0,2,1:T(8,128)(2,1)S(1)}, bf16[20,8,2,128]{3,0,2,1:T(8,128)(2,1)S(1)}, u32[]{:S(2)}, u32[]{:S(2)}) collective-permute-start(bf16[20,8,2,128]{3,0,2,1:T(8,128)(2,1)S(1)} %get-tuple-element.24), channel_id=1, source_target_pairs={{1,0},{2,1},{3,2},{4,3},{5,4},{6,5},{7,6},{8,7},{9,8},{10,9},{11,1... | collective-permute-start | bytes 245768 | tf_op jit(solution)/shard_map/ppermute | solution.py:21
Sparse Core Ops, SparseCore 0:
  11.9 111.7 all-gather.3
  137.7 92.0 all-gather.5
where the time goes:
time: 270 us; the launch traced here: 269 us
  waiting for transfers between devices  160 us (59%)
  starting transfers between devices  27.1 us (10%)
  blocking collectives  25.1 us (9%)
  matrix products  17 us (6%)
  between operations  16.3 us (6%)
  local copies, waits for them, and re-layouts  14.8 us (5%)
  other arithmetic  9.29 us (3%)
    all_gather x1, waiting for transfers between devices, body(): piece = lax.all_gather(outgoing, 'gx', axis=0, tiled=True)  79.9 us
    all_gather x1, waiting for transfers between devices, body(): piece = lax.all_gather(replies, 'gx', axis=0, tiled=True)  67.2 us
    unnamed x1, blocking collectives  25.1 us
    ppermute x4, starting transfers between devices, padded_2(): after = lax.ppermute(leading, axis, down)  16.1 us
    ppermute x4, waiting for transfers between devices, padded_2(): after = lax.ppermute(leading, axis, down)  12.5 us
    ppermute x4, starting transfers between devices, padded_2(): before = lax.ppermute(last, axis, up)  10.9 us
    unnamed x21, local copies, waits for them, and re-layouts  7.8 us
    dot_general x1, matrix products, network(): jnp.einsum('bzh,hk->bzk', hidden, w_mid, preferred_element_type=jnp.float32)  6.67 us
  transfers between devices with their start and end apart: 10, of which 6 were waited for; matrix products, arithmetic and copies ran while one was open for 6% of the time, Pallas kernels for 0%

commit v1 on v0

v1 whole, which is shorter than its diff:
```python
import jax
import jax.numpy as jnp
from jax import lax
from jax.sharding import PartitionSpec as P

step_size = 0.05
reaction_gain = 8.0
velocity_x = 1.0
velocity_y = -0.6
velocity_z = 0.35


def padded_2(x, sides, width):
    for axis, dim in sides:
        peers, length = (lax.axis_size(axis), x.shape[dim])
        up = [(i, (i + 1) % peers) for i in range(peers)]
        down = [(j, i) for i, j in up]
        last = lax.slice_in_dim(x, length - width, length, axis=dim)
        leading = lax.slice_in_dim(x, 0, width, axis=dim)
        before = lax.ppermute(last, axis, up)
        after = lax.ppermute(leading, axis, down)
        x = jnp.concatenate([before, x, after], axis=dim)
    return x


def stencil(shifted):
    plus_one = shifted(1)
    plus_two = shifted(2)
    minus_one = shifted(-1)
    minus_two = shifted(-2)
    slope = (8.0 * (plus_one - minus_one) - (plus_two - minus_two)) / 12.0
    curve = (16.0 * (plus_one + minus_one) - (plus_two + minus_two) - 30.0 * shifted(0)) / 12.0
    return (slope, curve)


def transport(field_set, diffusivity):
    wide_x = field_set.shape[1]
    wide_y = field_set.shape[2]
    padded = padded_2(field_set.astype(jnp.bfloat16), (("gx", 1), ("gy", 2)), 2).astype(
        field_set.dtype
    )
    slope_x, curve_x = stencil(
        lambda step_k: padded[:, 2 + step_k : 2 + step_k + wide_x, 2 : 2 + wide_y, :]
    )
    slope_y, curve_y = stencil(
        lambda step_k: padded[:, 2 : 2 + wide_x, 2 + step_k : 2 + step_k + wide_y, :]
    )
    slope_z, curve_z = stencil(lambda step_k: jnp.roll(field_set, -step_k, axis=3))
    return -(velocity_x * slope_x + velocity_y * slope_y + velocity_z * slope_z) + diffusivity[
        :, None, None, None
    ] * (curve_x + curve_y + curve_z)


def network(cell_rows, w_in, w_mid, w_low, w_out):
    hidden = jax.nn.silu(
        jnp.einsum("bfz,fh->bzh", cell_rows, w_in, preferred_element_type=jnp.float32)
    ).astype(jnp.bfloat16)
    hidden = jax.nn.silu(
        jnp.einsum("bzh,hk->bzk", hidden, w_mid, preferred_element_type=jnp.float32)
    ).astype(jnp.bfloat16)
    hidden = jax.nn.silu(
        jnp.einsum("bzk,kj->bzj", hidden, w_low, preferred_element_type=jnp.float32)
    ).astype(jnp.bfloat16)
    return jnp.einsum("bzj,fj->bfz", hidden, w_out, preferred_element_type=jnp.float32).astype(
        jnp.bfloat16
    )


def body(flow_state, reacting, w_in, w_mid, w_low, w_out, diffusivity):
    fields, wide_x, wide_y, depth_z = flow_state.shape
    blocks = wide_x * wide_y
    share = 3 * blocks // 8
    spread = min(share, blocks - share)
    cap = min(blocks, share + spread)
    live_mask = reacting.reshape(blocks)
    local_rank = jnp.cumsum(live_mask) - live_mask
    keep_pick = (
        (local_rank[None, :] == jnp.arange(cap)[:, None]) & (live_mask[None, :] == 1)
    ).astype(jnp.bfloat16)
    rows = jnp.moveaxis(flow_state.reshape(fields, blocks, depth_z), 1, 0).astype(jnp.bfloat16)
    batch = jnp.einsum("qb,bfz->qfz", keep_pick, rows, preferred_element_type=jnp.float32).astype(
        jnp.bfloat16
    )
    results = network(batch, w_in, w_mid, w_low, w_out)
    source = jnp.einsum("qb,qfz->bfz", keep_pick, results, preferred_element_type=jnp.float32)
    reaction = jnp.moveaxis(source, 0, 1).reshape(fields, wide_x, wide_y, depth_z)

    def tendency(field_set):
        return transport(field_set, diffusivity) + reaction_gain * reaction

    first_section = flow_state + step_size * tendency(flow_state)
    return 0.5 * flow_state + 0.5 * (first_section + step_size * tendency(first_section))


def solution(mesh):
    in_specs = (P(None, "gx", "gy", None), P("gx", "gy"), P(), P(), P(), P(), P())
    out_specs = P(None, "gx", "gy", None)
    return jax.shard_map(body, mesh=mesh, in_specs=in_specs, out_specs=out_specs, check_vma=False)
```

time: 270 us -> 116 us (0.43)
  the two profiles are of different devices: /device:TPU:1 before, /device:TPU:8 now
where the time goes in v1:
time: 116 us; the launch traced here: 115 us
  starting transfers between devices  47.1 us (41%)
  matrix products  21.8 us (19%)
  waiting for transfers between devices  21.1 us (18%)
  local copies, waits for them, and re-layouts  17.7 us (15%)
  other arithmetic  7.25 us (6%)
    ppermute x4, starting transfers between devices, padded_2(): after = lax.ppermute(leading, axis, down)  39.4 us
    ppermute x4, waiting for transfers between devices, padded_2(): before = lax.ppermute(last, axis, up)  21 us
    dot_general x1, matrix products, network(): jnp.einsum('bzh,hk->bzk', hidden, w_mid, preferred_element_type=jnp.float32)  12.1 us
    slice x8, local copies, waits for them, and re-layouts, transport(): jnp.roll(field_set, -step_k, axis=3)  7.73 us
    ppermute x4, starting transfers between devices, padded_2(): before = lax.ppermute(last, axis, up)  7.68 us
    dot_general x1, matrix products, network(): jnp.einsum('bzj,fj->bfz', hidden, w_out, preferred_element_type=jnp.float32)  7.58 us
    unnamed x15, local copies, waits for them, and re-layouts  6.29 us
    another operation x2, other arithmetic  2.66 us
  transfers between devices with their start and end apart: 8, of which 4 were waited for; matrix products, arithmetic and copies ran while one was open for 35% of the time, Pallas kernels for 0%

profile of v1, /device:TPU:8, one launch (start us, length us, event | category | flops | bytes accessed | tf_op | source)
XLA Modules:
  0.0 115.2 jit_solution(14983101801502548686)
XLA Ops:
  0.0 1.1 copy.49
  1.2 0.7 fusion.46
  1.8 14.0 %collective-permute-start.1 = (bf16[20,2,6,128]{3,0,2,1:T(8,128)(2,1)}, bf16[20,2,6,128]{3,0,2,1:T(8,128)(2,1)}, u32[]{:S(2)}, u32[]{:S(2)}) collective-permute-start(bf16[20,2,6,128]{3,0,2,1:T(8,128)(2,1)} %get-tuple-element.30), channel_id=1, source_target_pairs={{32,0},{64,32},{96,64},{128,96},{160,128},{192,160},{224,192},{256... | collective-permute-start | bytes 184328 | tf_op jit(solution)/shard_map/ppermute | solution.py:21
  15.8 1.9 %collective-permute-start = (bf16[20,2,6,128]{3,0,2,1:T(8,128)(2,1)}, bf16[20,2,6,128]{3,0,2,1:T(8,128)(2,1)}, u32[]{:S(2)}, u32[]{:S(2)}) collective-permute-start(bf16[20,2,6,128]{3,0,2,1:T(8,128)(2,1)} %get-tuple-element.29), channel_id=1, source_target_pairs={{0,32},{32,64},{64,96},{96,128},{128,160},{160,192},{192,224},{224... | collective-permute-start | bytes 184328 | tf_op jit(solution)/shard_map/ppermute | solution.py:20
  17.7 1.4 %reshape.56 = s32[24,1]{1,0:T(8,128)} reshape(s32[4,6]{1,0:T(4,128)} %param.8) | data formatting | bytes 192 | tf_op jit(solution)/shard_map/reshape.35
  19.1 0.8 reshape.50
  19.8 1.9 %fusion.43 = (f32[20,4,6,126]{3,1,2,0:T(4,128)S(1)}, f32[20,4,6,126]{3,1,2,0:T(4,128)}) fusion(f32[20,4,6,128]{3,1,2,0:T(4,128)} %param.7), kind=kLoop, calls=%fused_computation.65 | loop fusion | bytes 967680 | tf_op jit(solution)/shard_map/jit(_roll_static)/slice | solution.py:48
  21.7 2.0 %fusion.44 = (f32[20,4,6,2]{3,1,2,0:T(4,128)}, f32[20,4,6,2]{3,1,2,0:T(4,128)}) fusion(f32[20,4,6,128]{3,1,2,0:T(4,128)} %param.7), kind=kLoop, calls=%fused_computation.66 | loop fusion | bytes 15360 | tf_op jit(solution)/shard_map/jit(_roll_static)/slice | solution.py:48
  23.7 1.3 %fusion.41 = (f32[20,4,6,127]{3,1,2,0:T(4,128)S(1)}, f32[20,4,6,127]{3,1,2,0:T(4,128)S(1)}) fusion(f32[20,4,6,128]{3,1,2,0:T(4,128)} %param.7), kind=kLoop, calls=%fused_computation.63 | loop fusion | bytes 975360 | tf_op jit(solution)/shard_map/jit(_roll_static)/slice | solution.py:48
  25.0 2.0 %fusion.42 = (f32[20,4,6,1]{3,1,2,0:T(4,128)}, f32[20,4,6,1]{3,1,2,0:T(4,128)}) fusion(f32[20,4,6,128]{3,1,2,0:T(4,128)} %param.7), kind=kLoop, calls=%fused_computation.64 | loop fusion | bytes 7680 | tf_op jit(solution)/shard_map/jit(_roll_static)/slice | solution.py:48
  27.0 1.3 %reduce-window.8 = s32[24,1]{1,0:T(8,128)} reduce-window(s32[24,1]{1,0:T(8,128)} %reshape.56, s32[]{:T(128)} %constant.40.clone.1), window={size=24x1 pad=23_0x0_0}, to_apply=%region_0.0 | reduce-window | flops 552 | bytes 196 | tf_op jit(solution)/shard_map/reduce-window.3
  28.3 1.3 %reduce = s32[24]{0:T(128)} reduce(s32[24,1]{1,0:T(8,128)} %reduce-window.8, s32[]{:T(128)} %constant.40.clone.1), dimensions={1}, to_apply=%reduce-window.8.reduce_sub_computation | reduce | bytes 196 | tf_op jit(solution)/shard_map/reduce-window.3
  29.7 0.6 sub.112
  30.3 0.9 fusion.19
  31.2 12.1 %fusion = f32[18,128,800]{1,2,0:T(8,128)} fusion(bf16[1600,800]{0,1:T(8,128)(2,1)S(1)} %copy-done, bf16[18,20,128]{2,0,1:T(8,128)(2,1)} %fusion.19, bf16[20,1600]{1,0:T(8,128)(2,1)} %param.9), kind=kOutput, calls=%fused_computation.2 | convolution fusion | flops 6064128000 | bytes 10088960 | tf_op jit(solution)/shard_map/bzh,hk->bzk/dot_general | solution.py:59
  43.4 7.6 %fusion.5 = bf16[18,128,20]{1,2,0:T(8,128)(2,1)} fusion(f32[18,128,800]{1,2,0:T(8,128)} %fusion, bf16[800,400]{0,1:T(8,128)(2,1)} %param.11, bf16[20,400]{1,0:T(8,128)(2,1)} %param.12), kind=kOutput, calls=%fused_computation.7 | convolution fusion | flops 1525248000 | bytes 8120960 | tf_op jit(solution)/shard_map/bzj,fj->bfz/dot_general | solution.py:64
  51.0 1.2 %fusion.6 = f32[20,24,128]{2,1,0:T(8,128)S(1)} fusion(bf16[18,128,20]{1,2,0:T(8,128)(2,1)} %fusion.5, s32[24]{0:T(128)S(1)} %sub.112, pred[24]{0:T(512)(128)(4,1)S(1)} %broadcast_compare_fusion), kind=kOutput, calls=%fused_computation.9 | convolution fusion | flops 2274144 | bytes 338040 | tf_op jit(solution)/shard_map/qb,qfz->bfz/dot_general | solution.py:85
  52.1 0.0 collective-permute-done
  52.1 0.8 pad_maximum_fusion.13
  53.0 11.6 %collective-permute-start.3 = (bf16[20,8,2,128]{3,0,2,1:T(8,128)(2,1)S(1)}, bf16[20,8,2,128]{3,0,2,1:T(8,128)(2,1)S(1)}, u32[]{:S(2)}, u32[]{:S(2)}) collective-permute-start(bf16[20,8,2,128]{3,0,2,1:T(8,128)(2,1)S(1)} %get-tuple-element.18), channel_id=1, source_target_pairs={{1,0},{2,1},{3,2},{4,3},{5,4},{6,5},{7,6},{8,7},{9,8},{10,9},{11,1... | collective-permute-start | bytes 245768 | tf_op jit(solution)/shard_map/ppermute | solution.py:21
  64.6 1.9 %collective-permute-start.2 = (bf16[20,8,2,128]{3,0,2,1:T(8,128)(2,1)S(1)}, bf16[20,8,2,128]{3,0,2,1:T(8,128)(2,1)S(1)}, u32[]{:S(2)}, u32[]{:S(2)}) collective-permute-start(bf16[20,8,2,128]{3,0,2,1:T(8,128)(2,1)S(1)} %get-tuple-element.17), channel_id=1, source_target_pairs={{0,1},{1,2},{2,3},{3,4},{4,5},{5,6},{6,7},{7,8},{8,9},{9,10},{10,1... | collective-permute-start | bytes 245768 | tf_op jit(solution)/shard_map/ppermute | solution.py:20
  66.5 0.7 broadcast_multiply_fusion
  67.2 0.1 copy.22
  67.3 1.0 copy.41
  68.3 1.0 copy.42
  69.3 1.0 copy.43
  70.3 0.1 copy.44
  70.3 0.1 copy.45
  70.4 1.0 copy.46
  71.4 1.0 copy.47
  72.4 0.1 copy.48
  72.4 3.1 %collective-permute-done.2 = bf16[20,8,2,128]{3,0,2,1:T(8,128)(2,1)S(1)} collective-permute-done((bf16[20,8,2,128]{3,0,2,1:T(8,128)(2,1)S(1)}, bf16[20,8,2,128]{3,0,2,1:T(8,128)(2,1)S(1)}, u32[]{:S(2)}, u32[]{:S(2)}) %collective-permute-start.2) | collective-permute-done | bytes 81952 | tf_op jit(solution)/shard_map/ppermute | solution.py:20
  75.5 1.0 maximum_convert_fusion
  76.6 0.6 fusion.35
  77.2 0.1 fusion.39
  77.4 0.1 fusion.40
  77.6 7.7 %collective-permute-start.5 = (bf16[20,2,6,128]{3,0,2,1:T(8,128)(2,1)S(1)}, bf16[20,2,6,128]{3,0,2,1:T(8,128)(2,1)S(1)}, u32[]{:S(2)}, u32[]{:S(2)}) collective-permute-start(bf16[20,2,6,128]{3,0,2,1:T(8,128)(2,1)S(1)} %get-tuple-element.28), channel_id=1, source_target_pairs={{32,0},{64,32},{96,64},{128,96},{160,128},{192,160},{224,192},{256... | collective-permute-start | bytes 184328 | tf_op jit(solution)/shard_map/ppermute | solution.py:21
  85.3 1.9 %collective-permute-start.4 = (bf16[20,2,6,128]{3,0,2,1:T(8,128)(2,1)S(1)}, bf16[20,2,6,128]{3,0,2,1:T(8,128)(2,1)S(1)}, u32[]{:S(2)}, u32[]{:S(2)}) collective-permute-start(bf16[20,2,6,128]{3,0,2,1:T(8,128)(2,1)S(1)} %get-tuple-element.27), channel_id=1, source_target_pairs={{0,32},{32,64},{64,96},{96,128},{128,160},{160,192},{192,224},{224... | collective-permute-start | bytes 184328 | tf_op jit(solution)/shard_map/ppermute | solution.py:20
  87.2 0.1 fusion.37
  87.4 9.7 %collective-permute-done.4 = bf16[20,2,6,128]{3,0,2,1:T(8,128)(2,1)S(1)} collective-permute-done((bf16[20,2,6,128]{3,0,2,1:T(8,128)(2,1)S(1)}, bf16[20,2,6,128]{3,0,2,1:T(8,128)(2,1)S(1)}, u32[]{:S(2)}, u32[]{:S(2)}) %collective-permute-start.4) | collective-permute-done | bytes 61472 | tf_op jit(solution)/shard_map/ppermute | solution.py:20
  97.1 6.1 %collective-permute-start.7 = (bf16[20,8,2,128]{3,0,2,1:T(8,128)(2,1)S(1)}, bf16[20,8,2,128]{3,0,2,1:T(8,128)(2,1)S(1)}, u32[]{:S(2)}, u32[]{:S(2)}) collective-permute-start(bf16[20,8,2,128]{3,0,2,1:T(8,128)(2,1)S(1)} %get-tuple-element.16), channel_id=1, source_target_pairs={{1,0},{2,1},{3,2},{4,3},{5,4},{6,5},{7,6},{8,7},{9,8},{10,9},{11,1... | collective-permute-start | bytes 245768 | tf_op jit(solution)/shard_map/ppermute | solution.py:21
  103.2 1.9 %collective-permute-start.6 = (bf16[20,8,2,128]{3,0,2,1:T(8,128)(2,1)S(1)}, bf16[20,8,2,128]{3,0,2,1:T(8,128)(2,1)S(1)}, u32[]{:S(2)}, u32[]{:S(2)}) collective-permute-start(bf16[20,8,2,128]{3,0,2,1:T(8,128)(2,1)S(1)} %get-tuple-element.15), channel_id=1, source_target_pairs={{0,1},{1,2},{2,3},{3,4},{4,5},{5,6},{6,7},{7,8},{8,9},{9,10},{10,1... | collective-permute-start | bytes 245768 | tf_op jit(solution)/shard_map/ppermute | solution.py:20
  105.1 0.1 fusion.38
  105.3 0.1 collective-permute-done.7
  105.4 8.2 %collective-permute-done.6 = bf16[20,8,2,128]{3,0,2,1:T(8,128)(2,1)S(1)} collective-permute-done((bf16[20,8,2,128]{3,0,2,1:T(8,128)(2,1)S(1)}, bf16[20,8,2,128]{3,0,2,1:T(8,128)(2,1)S(1)}, u32[]{:S(2)}, u32[]{:S(2)}) %collective-permute-start.6) | collective-permute-done | bytes 81952 | tf_op jit(solution)/shard_map/ppermute | solution.py:20
  113.6 0.1 maximum_convert_fusion.1
  113.7 0.7 fusion.13
  114.4 0.8 copy.25
  (12 shorter events, 0.1 us)
Async XLA Ops:
  0.0 31.2 %copy-start = (bf16[1600,800]{0,1:T(8,128)(2,1)S(1)}, bf16[1600,800]{0,1:T(8,128)(2,1)}, u32[]{:S(2)}) copy-start(bf16[1600,800]{0,1:T(8,128)(2,1)} %param.10) | copy-start | bytes 7680004
  1.8 50.3 %collective-permute-start.1 = (bf16[20,2,6,128]{3,0,2,1:T(8,128)(2,1)}, bf16[20,2,6,128]{3,0,2,1:T(8,128)(2,1)}, u32[]{:S(2)}, u32[]{:S(2)}) collective-permute-start(bf16[20,2,6,128]{3,0,2,1:T(8,128)(2,1)} %get-tuple-element.30), channel_id=1, source_target_pairs={{32,0},{64,32},{96,64},{128,96},{160,128},{192,160},{224,192},{256... | collective-permute-start | bytes 184328 | tf_op jit(solution)/shard_map/ppermute | solution.py:21
  15.8 36.4 %collective-permute-start = (bf16[20,2,6,128]{3,0,2,1:T(8,128)(2,1)}, bf16[20,2,6,128]{3,0,2,1:T(8,128)(2,1)}, u32[]{:S(2)}, u32[]{:S(2)}) collective-permute-start(bf16[20,2,6,128]{3,0,2,1:T(8,128)(2,1)} %get-tuple-element.29), channel_id=1, source_target_pairs={{0,32},{32,64},{64,96},{96,128},{128,160},{160,192},{192,224},{224... | collective-permute-start | bytes 184328 | tf_op jit(solution)/shard_map/ppermute | solution.py:20
  19.8 9.8 %copy-start.2 = (s32[24]{0:T(128)}, s32[24]{0:T(128)S(1)}, u32[]{:S(2)}) copy-start(s32[24]{0:T(128)S(1)} %reshape.50) | copy-start | bytes 292
  50.9 25.6 %copy-start.1 = (f32[20,4,6,128]{3,1,2,0:T(4,128)S(1)}, f32[20,4,6,128]{3,1,2,0:T(4,128)}, u32[]{:S(2)}) copy-start(f32[20,4,6,128]{3,1,2,0:T(4,128)} %param.7) | copy-start | bytes 737284
  53.0 19.5 %collective-permute-start.3 = (bf16[20,8,2,128]{3,0,2,1:T(8,128)(2,1)S(1)}, bf16[20,8,2,128]{3,0,2,1:T(8,128)(2,1)S(1)}, u32[]{:S(2)}, u32[]{:S(2)}) collective-permute-start(bf16[20,8,2,128]{3,0,2,1:T(8,128)(2,1)S(1)} %get-tuple-element.18), channel_id=1, source_target_pairs={{1,0},{2,1},{3,2},{4,3},{5,4},{6,5},{7,6},{8,7},{9,8},{10,9},{11,1... | collective-permute-start | bytes 245768 | tf_op jit(solution)/shard_map/ppermute | solution.py:21
  64.6 10.9 %collective-permute-start.2 = (bf16[20,8,2,128]{3,0,2,1:T(8,128)(2,1)S(1)}, bf16[20,8,2,128]{3,0,2,1:T(8,128)(2,1)S(1)}, u32[]{:S(2)}, u32[]{:S(2)}) collective-permute-start(bf16[20,8,2,128]{3,0,2,1:T(8,128)(2,1)S(1)} %get-tuple-element.17), channel_id=1, source_target_pairs={{0,1},{1,2},{2,3},{3,4},{4,5},{5,6},{6,7},{7,8},{8,9},{9,10},{10,1... | collective-permute-start | bytes 245768 | tf_op jit(solution)/shard_map/ppermute | solution.py:20
  77.6 9.8 %collective-permute-start.5 = (bf16[20,2,6,128]{3,0,2,1:T(8,128)(2,1)S(1)}, bf16[20,2,6,128]{3,0,2,1:T(8,128)(2,1)S(1)}, u32[]{:S(2)}, u32[]{:S(2)}) collective-permute-start(bf16[20,2,6,128]{3,0,2,1:T(8,128)(2,1)S(1)} %get-tuple-element.28), channel_id=1, source_target_pairs={{32,0},{64,32},{96,64},{128,96},{160,128},{192,160},{224,192},{256... | collective-permute-start | bytes 184328 | tf_op jit(solution)/shard_map/ppermute | solution.py:21
  85.3 11.8 %collective-permute-start.4 = (bf16[20,2,6,128]{3,0,2,1:T(8,128)(2,1)S(1)}, bf16[20,2,6,128]{3,0,2,1:T(8,128)(2,1)S(1)}, u32[]{:S(2)}, u32[]{:S(2)}) collective-permute-start(bf16[20,2,6,128]{3,0,2,1:T(8,128)(2,1)S(1)} %get-tuple-element.27), channel_id=1, source_target_pairs={{0,32},{32,64},{64,96},{96,128},{128,160},{160,192},{192,224},{224... | collective-permute-start | bytes 184328 | tf_op jit(solution)/shard_map/ppermute | solution.py:20
  97.1 8.3 %collective-permute-start.7 = (bf16[20,8,2,128]{3,0,2,1:T(8,128)(2,1)S(1)}, bf16[20,8,2,128]{3,0,2,1:T(8,128)(2,1)S(1)}, u32[]{:S(2)}, u32[]{:S(2)}) collective-permute-start(bf16[20,8,2,128]{3,0,2,1:T(8,128)(2,1)S(1)} %get-tuple-element.16), channel_id=1, source_target_pairs={{1,0},{2,1},{3,2},{4,3},{5,4},{6,5},{7,6},{8,7},{9,8},{10,9},{11,1... | collective-permute-start | bytes 245768 | tf_op jit(solution)/shard_map/ppermute | solution.py:21
  103.2 10.4 %collective-permute-start.6 = (bf16[20,8,2,128]{3,0,2,1:T(8,128)(2,1)S(1)}, bf16[20,8,2,128]{3,0,2,1:T(8,128)(2,1)S(1)}, u32[]{:S(2)}, u32[]{:S(2)}) collective-permute-start(bf16[20,8,2,128]{3,0,2,1:T(8,128)(2,1)S(1)} %get-tuple-element.15), channel_id=1, source_target_pairs={{0,1},{1,2},{2,3},{3,4},{4,5},{5,6},{6,7},{7,8},{8,9},{9,10},{10,1... | collective-permute-start | bytes 245768 | tf_op jit(solution)/shard_map/ppermute | solution.py:20

commit v2 on v1

--- a/solution.py
+++ b/solution.py
@@ -1,5 +1,6 @@
 import jax
 import jax.numpy as jnp
+import numpy as np
 from jax import lax
 from jax.sharding import PartitionSpec as P
 
@@ -10,17 +11,27 @@
 velocity_z = 0.35
 
 
-def padded_2(x, sides, width):
-    for axis, dim in sides:
-        peers, length = (lax.axis_size(axis), x.shape[dim])
-        up = [(i, (i + 1) % peers) for i in range(peers)]
-        down = [(j, i) for i, j in up]
-        last = lax.slice_in_dim(x, length - width, length, axis=dim)
-        leading = lax.slice_in_dim(x, 0, width, axis=dim)
-        before = lax.ppermute(last, axis, up)
-        after = lax.ppermute(leading, axis, down)
-        x = jnp.concatenate([before, x, after], axis=dim)
-    return x
+def ring(axis, step):
+    peers = lax.axis_size(axis)
+    return [(i, (i + step) % peers) for i in range(peers)]
+
+
+def halos(x):
+    wide_x, wide_y = x.shape[1], x.shape[2]
+    low = x.astype(jnp.bfloat16)
+    x_before = lax.ppermute(low[:, wide_x - 2 :], "gx", ring("gx", 1))
+    x_after = lax.ppermute(low[:, :2], "gx", ring("gx", -1))
+    y_before = lax.ppermute(low[:, :, wide_y - 2 :], "gy", ring("gy", 1))
+    y_after = lax.ppermute(low[:, :, :2], "gy", ring("gy", -1))
+    return x_before, x_after, y_before, y_after
+
+
+def circulant(depth, taps):
+    m = np.zeros((depth, depth), np.float32)
+    for k, c in taps.items():
+        for z in range(depth):
+            m[(z + k) % depth, z] += c
+    return jnp.asarray(m)
 
 
 def stencil(shifted):
@@ -36,16 +47,17 @@
 def transport(field_set, diffusivity):
     wide_x = field_set.shape[1]
     wide_y = field_set.shape[2]
-    padded = padded_2(field_set.astype(jnp.bfloat16), (("gx", 1), ("gy", 2)), 2).astype(
-        field_set.dtype
-    )
-    slope_x, curve_x = stencil(
-        lambda step_k: padded[:, 2 + step_k : 2 + step_k + wide_x, 2 : 2 + wide_y, :]
-    )
-    slope_y, curve_y = stencil(
-        lambda step_k: padded[:, 2 : 2 + wide_x, 2 + step_k : 2 + step_k + wide_y, :]
-    )
-    slope_z, curve_z = stencil(lambda step_k: jnp.roll(field_set, -step_k, axis=3))
+    depth = field_set.shape[3]
+    x_before, x_after, y_before, y_after = halos(field_set)
+    dtype = field_set.dtype
+    pad_x = jnp.concatenate([x_before.astype(dtype), field_set, x_after.astype(dtype)], axis=1)
+    pad_y = jnp.concatenate([y_before.astype(dtype), field_set, y_after.astype(dtype)], axis=2)
+    slope_x, curve_x = stencil(lambda k: pad_x[:, 2 + k : 2 + k + wide_x])
+    slope_y, curve_y = stencil(lambda k: pad_y[:, :, 2 + k : 2 + k + wide_y])
+    slope_m = circulant(depth, {1: 8.0, -1: -8.0, 2: -1.0, -2: 1.0})
+    curve_m = circulant(depth, {1: 16.0, -1: 16.0, 2: -1.0, -2: -1.0, 0: -30.0})
+    slope_z = jnp.einsum("fxyz,zw->fxyw", field_set, slope_m, precision=lax.Precision.HIGHEST) / 12.0
+    curve_z = jnp.einsum("fxyz,zw->fxyw", field_set, curve_m, precision=lax.Precision.HIGHEST) / 12.0
     return -(velocity_x * slope_x + velocity_y * slope_y + velocity_z * slope_z) + diffusivity[
         :, None, None, None
     ] * (curve_x + curve_y + curve_z)
@@ -73,7 +85,8 @@
     spread = min(share, blocks - share)
     cap = min(blocks, share + spread)
     live_mask = reacting.reshape(blocks)
-    local_rank = jnp.cumsum(live_mask) - live_mask
+    order = jnp.arange(blocks)
+    local_rank = jnp.sum(jnp.where(order[None, :] < order[:, None], live_mask[None, :], 0), axis=1)
     keep_pick = (
         (local_rank[None, :] == jnp.arange(cap)[:, None]) & (live_mask[None, :] == 1)
     ).astype(jnp.bfloat16)

time: 116 us -> 85.5 us (0.74)
  local copies, waits for them, and re-layouts: 17.7 us -> 2.89 us
  waiting for transfers between devices: 21.1 us -> 7.95 us
  other arithmetic: 7.25 us -> 0.21 us
  starting transfers between devices: 47.1 us -> 50.2 us
  matrix products: 21.8 us -> 23.4 us
    ppermute x8, waiting for transfers between devices: 21.1 us -> 7.95 us  [the longest x2 7.94 us: halos(): y_before = lax.ppermute(low[:, :, wide_y - 2:], 'gy', ring('gy', 1))]
    slice x10 -> x4, local copies, waits for them, and re-layouts: 8.42 us -> 0.06 us  [the longest x2 0.03 us: halos(): x_before = lax.ppermute(low[:, wide_x - 2:], 'gx', ring('gx', 1))]
    unnamed x15 -> x14, local copies, waits for them, and re-layouts: 6.29 us -> 1.23 us
    dot_general x0 -> x4, matrix products: none -> 3.67 us  [the longest x2 1.93 us: transport(): jnp.einsum('fxyz,zw->fxyw', field_set, slope_m, precision=lax.Precision.H...]
    ppermute x8, starting transfers between devices: 47.1 us -> 50.2 us  [the longest x2 21.9 us: halos(): y_after = lax.ppermute(low[:, :, :2], 'gy', ring('gy', -1))]
    another operation x2 -> x0, other arithmetic: 2.66 us -> none
    another operation x2 -> x0, local copies, waits for them, and re-layouts: 2.12 us -> none
    convert_element_type x3 -> x8, other arithmetic: 1.8 us -> 0.09 us  [the longest x2 0.03 us: transport(): x_after.astype(dtype)]
  transfers between devices with their start and end apart: 8 -> 8, of which waited for: 4 -> 1; matrix products, arithmetic and copies ran while one was open for 35% -> 24% of each run, Pallas kernels for 0% -> 0%
where the time goes in v2:
time: 85.5 us; the launch traced here: 85 us
  starting transfers between devices  50.2 us (59%)
  matrix products  23.4 us (27%)
  waiting for transfers between devices  7.95 us (9%)
  local copies, waits for them, and re-layouts  2.89 us (3%)
    ppermute x2, starting transfers between devices, halos(): y_after = lax.ppermute(low[:, :, :2], 'gy', ring('gy', -1))  21.9 us
    ppermute x2, starting transfers between devices, halos(): x_after = lax.ppermute(low[:, :2], 'gx', ring('gx', -1))  20.7 us
    dot_general x1, matrix products, network(): jnp.einsum('bzh,hk->bzk', hidden, w_mid, preferred_element_type=jnp.float32)  12.1 us
    ppermute x2, waiting for transfers between devices, halos(): y_before = lax.ppermute(low[:, :, wide_y - 2:], 'gy', ring('gy', 1))  7.94 us
    dot_general x1, matrix products, network(): jnp.einsum('bzj,fj->bfz', hidden, w_out, preferred_element_type=jnp.float32)  7.1 us
    ppermute x2, starting transfers between devices, halos(): y_before = lax.ppermute(low[:, :, wide_y - 2:], 'gy', ring('gy', 1))  3.84 us
    ppermute x2, starting transfers between devices, halos(): x_before = lax.ppermute(low[:, wide_x - 2:], 'gx', ring('gx', 1))  3.84 us
    dot_general x2, matrix products, transport(): jnp.einsum('fxyz,zw->fxyw', field_set, slope_m, precision=lax.Precision.H...  1.93 us
  transfers between devices with their start and end apart: 8, of which 1 were waited for; matrix products, arithmetic and copies ran while one was open for 24% of the time, Pallas kernels for 0%

profile of v2, /device:TPU:8, one launch (start us, length us, event | category | flops | bytes accessed | tf_op | source)
XLA Modules:
  0.0 85.0 jit_solution(12353311745577001121)
XLA Ops:
  0.0 0.0 copy-start
  0.0 1.1 %copy.52 = bf16[20,4,6,128]{3,0,2,1:T(8,128)(2,1)S(1)} copy(f32[20,4,6,128]{3,1,2,0:T(4,128)} %param.11) | data formatting | bytes 368640 | tf_op args[0]
  1.2 14.3 %collective-permute-start.2 = (bf16[20,4,2,128]{3,0,2,1:T(8,128)(2,1)S(1)}, bf16[20,4,2,128]{3,0,2,1:T(8,128)(2,1)S(1)}, u32[]{:S(2)}, u32[]{:S(2)}) collective-permute-start(bf16[20,4,2,128]{3,0,2,1:T(8,128)(2,1)S(1)} %get-tuple-element.12), channel_id=1, source_target_pairs={{0,31},{1,0},{2,1},{3,2},{4,3},{5,4},{6,5},{7,6},{8,7},{9,8},{10,9... | collective-permute-start | bytes 122888 | tf_op jit(solution)/shard_map/ppermute | solution.py:25
  15.5 1.9 %collective-permute-start.3 = (bf16[20,4,2,128]{3,0,2,1:T(8,128)(2,1)S(1)}, bf16[20,4,2,128]{3,0,2,1:T(8,128)(2,1)S(1)}, u32[]{:S(2)}, u32[]{:S(2)}) collective-permute-start(bf16[20,4,2,128]{3,0,2,1:T(8,128)(2,1)S(1)} %get-tuple-element.11), channel_id=1, source_target_pairs={{0,1},{1,2},{2,3},{3,4},{4,5},{5,6},{6,7},{7,8},{8,9},{9,10},{10,1... | collective-permute-start | bytes 122888 | tf_op jit(solution)/shard_map/ppermute | solution.py:24
  17.5 11.0 %collective-permute-start = (bf16[20,2,6,128]{3,0,2,1:T(8,128)(2,1)S(1)}, bf16[20,2,6,128]{3,0,2,1:T(8,128)(2,1)S(1)}, u32[]{:S(2)}, u32[]{:S(2)}) collective-permute-start(bf16[20,2,6,128]{3,0,2,1:T(8,128)(2,1)S(1)} %get-tuple-element.10), channel_id=1, source_target_pairs={{0,992},{32,0},{64,32},{96,64},{128,96},{160,128},{192,160},{224,1... | collective-permute-start | bytes 184328 | tf_op jit(solution)/shard_map/ppermute | solution.py:23
  28.5 1.9 %collective-permute-start.1 = (bf16[20,2,6,128]{3,0,2,1:T(8,128)(2,1)S(1)}, bf16[20,2,6,128]{3,0,2,1:T(8,128)(2,1)S(1)}, u32[]{:S(2)}, u32[]{:S(2)}) collective-permute-start(bf16[20,2,6,128]{3,0,2,1:T(8,128)(2,1)S(1)} %get-tuple-element.9), channel_id=1, source_target_pairs={{0,32},{32,64},{64,96},{96,128},{128,160},{160,192},{192,224},{224... | collective-permute-start | bytes 184328 | tf_op jit(solution)/shard_map/ppermute | solution.py:22
  30.4 0.8 broadcast_in_dim.20
  31.1 0.1 select_reduce_fusion
  31.3 0.3 fusion.37
  31.6 0.0 copy-done
  31.6 0.0 copy-start.2
  31.6 12.1 %fusion = f32[18,128,800]{1,2,0:T(8,128)} fusion(bf16[1600,800]{0,1:T(8,128)(2,1)S(1)} %copy-done, bf16[18,20,128]{2,0,1:T(8,128)(2,1)S(1)} %fusion.37, bf16[20,1600]{1,0:T(8,128)(2,1)} %param.13), kind=kOutput, calls=%fused_computation.2 | convolution fusion | flops 6064128000 | bytes 10088960 | tf_op jit(solution)/shard_map/bzh,hk->bzk/dot_general | solution.py:71
  43.7 0.0 copy-done.2
  43.7 0.0 copy-start.3
  43.7 0.0 copy-start.1
  43.7 7.1 %fusion.5 = bf16[18,128,20]{1,2,0:T(8,128)(2,1)S(1)} fusion(f32[18,128,800]{1,2,0:T(8,128)} %fusion, bf16[800,400]{0,1:T(8,128)(2,1)} %param.15, bf16[20,400]{1,0:T(8,128)(2,1)S(1)} %copy-done.2), kind=kOutput, calls=%fused_computation.7 | convolution fusion | flops 1525248000 | bytes 8120960 | tf_op jit(solution)/shard_map/bzj,fj->bfz/dot_general | solution.py:76
  50.8 0.0 copy-start.4
  50.8 0.0 copy-start.5
  50.8 0.2 fusion.24
  51.1 0.0 copy-done.3
  51.1 0.0 copy-done.1
  51.1 0.1 copy.34
  51.2 0.1 copy.32
  51.2 0.0 collective-permute-done.2
  51.3 0.0 collective-permute-done.3
  51.3 0.0 collective-permute-done
  51.3 0.0 collective-permute-done.1
  51.3 1.3 %fusion.15 = f32[20,4,6,128]{3,0,2,1:T(8,128)S(1)} fusion(f32[128,128,1,1]{1,0,3,2:T(8,128)} %constant.52, f32[20,4,6,128]{3,0,2,1:T(8,128)S(1)} %copy.34, f32[20,4,2,128]{3,0,2,1:T(8,128)S(1)} %convert_element_type.59, f32[20,4,2,128]{3,0,2,1:T(8,128)S(1)} %convert_element_type.60, f32[20,2,6,128]{3,0,2,1:T(8,128)S(1)} %convert_element_type.57, ...), kind=kOutput, calls=%fused_computation.21 | convolution fusion | flops 95723520 | bytes 1393152 | tf_op jit(solution)/shard_map/fxyz,zw->fxyw/dot_general | solution.py:60
  52.6 1.3 %fusion.57 = (bf16[20,4,6,128]{3,0,2,1:T(8,128)(2,1)S(1)}, f32[20,4,6,128]{3,0,2,1:T(8,128)S(1)}) fusion(f32[20,4,6,128]{3,0,2,1:T(8,128)S(1)} %copy.34, f32[20,4,6,128]{3,0,2,1:T(8,128)S(1)} %bitcast.62, f32[20,4,6,128]{3,0,2,1:T(8,128)S(1)} %fusion.15, f32[128,128,1,1]{1,0,3,2:T(8,128)} %constant.51, f32[20,4,2,128]{3,0,2,1:T(8,128)S(1)} %convert_element_type.60, ...), kind=kOutput, calls=%fused_computation.90 | convolution fusion | flops 96030720 | bytes 2105344 | tf_op jit(solution)/shard_map/fxyz,zw->fxyw/dot_general | solution.py:59
  54.0 9.7 %collective-permute-start.4 = (bf16[20,2,6,128]{3,0,2,1:T(8,128)(2,1)S(1)}, bf16[20,2,6,128]{3,0,2,1:T(8,128)(2,1)S(1)}, u32[]{:S(2)}, u32[]{:S(2)}) collective-permute-start(bf16[20,2,6,128]{3,0,2,1:T(8,128)(2,1)S(1)} %get-tuple-element.6), channel_id=1, source_target_pairs={{0,992},{32,0},{64,32},{96,64},{128,96},{160,128},{192,160},{224,1... | collective-permute-start | bytes 184328 | tf_op jit(solution)/shard_map/ppermute | solution.py:23
  63.7 1.9 %collective-permute-start.5 = (bf16[20,2,6,128]{3,0,2,1:T(8,128)(2,1)S(1)}, bf16[20,2,6,128]{3,0,2,1:T(8,128)(2,1)S(1)}, u32[]{:S(2)}, u32[]{:S(2)}) collective-permute-start(bf16[20,2,6,128]{3,0,2,1:T(8,128)(2,1)S(1)} %get-tuple-element.5), channel_id=1, source_target_pairs={{0,32},{32,64},{64,96},{96,128},{128,160},{160,192},{192,224},{224... | collective-permute-start | bytes 184328 | tf_op jit(solution)/shard_map/ppermute | solution.py:22
  65.6 7.6 %collective-permute-start.6 = (bf16[20,4,2,128]{3,0,2,1:T(8,128)(2,1)S(1)}, bf16[20,4,2,128]{3,0,2,1:T(8,128)(2,1)S(1)}, u32[]{:S(2)}, u32[]{:S(2)}) collective-permute-start(bf16[20,4,2,128]{3,0,2,1:T(8,128)(2,1)S(1)} %get-tuple-element.8), channel_id=1, source_target_pairs={{0,31},{1,0},{2,1},{3,2},{4,3},{5,4},{6,5},{7,6},{8,7},{9,8},{10,9... | collective-permute-start | bytes 122888 | tf_op jit(solution)/shard_map/ppermute | solution.py:25
  73.2 1.9 %collective-permute-start.7 = (bf16[20,4,2,128]{3,0,2,1:T(8,128)(2,1)S(1)}, bf16[20,4,2,128]{3,0,2,1:T(8,128)(2,1)S(1)}, u32[]{:S(2)}, u32[]{:S(2)}) collective-permute-start(bf16[20,4,2,128]{3,0,2,1:T(8,128)(2,1)S(1)} %get-tuple-element.7), channel_id=1, source_target_pairs={{0,1},{1,2},{2,3},{3,4},{4,5},{5,6},{6,7},{7,8},{8,9},{9,10},{10,1... | collective-permute-start | bytes 122888 | tf_op jit(solution)/shard_map/ppermute | solution.py:24
  75.1 0.0 collective-permute-done.6
  75.2 7.9 %collective-permute-done.7 = bf16[20,4,2,128]{3,0,2,1:T(8,128)(2,1)S(1)} collective-permute-done((bf16[20,4,2,128]{3,0,2,1:T(8,128)(2,1)S(1)}, bf16[20,4,2,128]{3,0,2,1:T(8,128)(2,1)S(1)}, u32[]{:S(2)}, u32[]{:S(2)}) %collective-permute-start.7) | collective-permute-done | bytes 40992 | tf_op jit(solution)/shard_map/ppermute | solution.py:24
  83.1 0.0 collective-permute-done.4
  83.1 0.0 collective-permute-done.5
  83.2 0.0 copy-done.4
  83.2 0.5 fusion.6
  83.6 0.0 copy-done.5
  83.6 0.6 fusion.20
  84.2 0.8 copy.35
  (14 shorter events, 0.2 us)
Async XLA Ops:
  0.0 31.6 %copy-start = (bf16[1600,800]{0,1:T(8,128)(2,1)S(1)}, bf16[1600,800]{0,1:T(8,128)(2,1)}, u32[]{:S(2)}) copy-start(bf16[1600,800]{0,1:T(8,128)(2,1)} %param.14) | copy-start | bytes 7680004
  1.2 50.1 %collective-permute-start.2 = (bf16[20,4,2,128]{3,0,2,1:T(8,128)(2,1)S(1)}, bf16[20,4,2,128]{3,0,2,1:T(8,128)(2,1)S(1)}, u32[]{:S(2)}, u32[]{:S(2)}) collective-permute-start(bf16[20,4,2,128]{3,0,2,1:T(8,128)(2,1)S(1)} %get-tuple-element.12), channel_id=1, source_target_pairs={{0,31},{1,0},{2,1},{3,2},{4,3},{5,4},{6,5},{7,6},{8,7},{9,8},{10,9... | collective-permute-start | bytes 122888 | tf_op jit(solution)/shard_map/ppermute | solution.py:25
  15.5 35.8 %collective-permute-start.3 = (bf16[20,4,2,128]{3,0,2,1:T(8,128)(2,1)S(1)}, bf16[20,4,2,128]{3,0,2,1:T(8,128)(2,1)S(1)}, u32[]{:S(2)}, u32[]{:S(2)}) collective-permute-start(bf16[20,4,2,128]{3,0,2,1:T(8,128)(2,1)S(1)} %get-tuple-element.11), channel_id=1, source_target_pairs={{0,1},{1,2},{2,3},{3,4},{4,5},{5,6},{6,7},{7,8},{8,9},{9,10},{10,1... | collective-permute-start | bytes 122888 | tf_op jit(solution)/shard_map/ppermute | solution.py:24
  17.5 33.8 %collective-permute-start = (bf16[20,2,6,128]{3,0,2,1:T(8,128)(2,1)S(1)}, bf16[20,2,6,128]{3,0,2,1:T(8,128)(2,1)S(1)}, u32[]{:S(2)}, u32[]{:S(2)}) collective-permute-start(bf16[20,2,6,128]{3,0,2,1:T(8,128)(2,1)S(1)} %get-tuple-element.10), channel_id=1, source_target_pairs={{0,992},{32,0},{64,32},{96,64},{128,96},{160,128},{192,160},{224,1... | collective-permute-start | bytes 184328 | tf_op jit(solution)/shard_map/ppermute | solution.py:23
  28.5 22.9 %collective-permute-start.1 = (bf16[20,2,6,128]{3,0,2,1:T(8,128)(2,1)S(1)}, bf16[20,2,6,128]{3,0,2,1:T(8,128)(2,1)S(1)}, u32[]{:S(2)}, u32[]{:S(2)}) collective-permute-start(bf16[20,2,6,128]{3,0,2,1:T(8,128)(2,1)S(1)} %get-tuple-element.9), channel_id=1, source_target_pairs={{0,32},{32,64},{64,96},{96,128},{128,160},{160,192},{192,224},{224... | collective-permute-start | bytes 184328 | tf_op jit(solution)/shard_map/ppermute | solution.py:22
  31.6 12.1 %copy-start.2 = (bf16[20,400]{1,0:T(8,128)(2,1)S(1)}, bf16[20,400]{1,0:T(8,128)(2,1)}, u32[]{:S(2)}) copy-start(bf16[20,400]{1,0:T(8,128)(2,1)} %param.16) | copy-start | bytes 48004
  43.7 7.4 %copy-start.3 = (f32[20]{0:T(128)S(1)}, f32[20]{0:T(128)}, u32[]{:S(2)}) copy-start(f32[20]{0:T(128)} %param.17) | copy-start | bytes 244
  43.7 7.4 %copy-start.1 = (f32[20,4,6,128]{3,1,2,0:T(4,128)S(1)}, f32[20,4,6,128]{3,1,2,0:T(4,128)}, u32[]{:S(2)}) copy-start(f32[20,4,6,128]{3,1,2,0:T(4,128)} %param.11) | copy-start | bytes 737284
  50.8 32.3 %copy-start.4 = (f32[128,128,1,1]{1,0,3,2:T(8,128)S(1)}, f32[128,128,1,1]{1,0,3,2:T(8,128)}, u32[]{:S(2)}) copy-start(f32[128,128,1,1]{1,0,3,2:T(8,128)} %constant.52) | copy-start | bytes 196612
  50.8 32.8 %copy-start.5 = (f32[128,128,1,1]{1,0,3,2:T(8,128)S(1)}, f32[128,128,1,1]{1,0,3,2:T(8,128)}, u32[]{:S(2)}) copy-start(f32[128,128,1,1]{1,0,3,2:T(8,128)} %constant.51) | copy-start | bytes 196612
  54.0 29.1 %collective-permute-start.4 = (bf16[20,2,6,128]{3,0,2,1:T(8,128)(2,1)S(1)}, bf16[20,2,6,128]{3,0,2,1:T(8,128)(2,1)S(1)}, u32[]{:S(2)}, u32[]{:S(2)}) collective-permute-start(bf16[20,2,6,128]{3,0,2,1:T(8,128)(2,1)S(1)} %get-tuple-element.6), channel_id=1, source_target_pairs={{0,992},{32,0},{64,32},{96,64},{128,96},{160,128},{192,160},{224,1... | collective-permute-start | bytes 184328 | tf_op jit(solution)/shard_map/ppermute | solution.py:23
  63.7 19.4 %collective-permute-start.5 = (bf16[20,2,6,128]{3,0,2,1:T(8,128)(2,1)S(1)}, bf16[20,2,6,128]{3,0,2,1:T(8,128)(2,1)S(1)}, u32[]{:S(2)}, u32[]{:S(2)}) collective-permute-start(bf16[20,2,6,128]{3,0,2,1:T(8,128)(2,1)S(1)} %get-tuple-element.5), channel_id=1, source_target_pairs={{0,32},{32,64},{64,96},{96,128},{128,160},{160,192},{192,224},{224... | collective-permute-start | bytes 184328 | tf_op jit(solution)/shard_map/ppermute | solution.py:22
  65.6 9.5 %collective-permute-start.6 = (bf16[20,4,2,128]{3,0,2,1:T(8,128)(2,1)S(1)}, bf16[20,4,2,128]{3,0,2,1:T(8,128)(2,1)S(1)}, u32[]{:S(2)}, u32[]{:S(2)}) collective-permute-start(bf16[20,4,2,128]{3,0,2,1:T(8,128)(2,1)S(1)} %get-tuple-element.8), channel_id=1, source_target_pairs={{0,31},{1,0},{2,1},{3,2},{4,3},{5,4},{6,5},{7,6},{8,7},{9,8},{10,9... | collective-permute-start | bytes 122888 | tf_op jit(solution)/shard_map/ppermute | solution.py:25
  73.2 9.9 %collective-permute-start.7 = (bf16[20,4,2,128]{3,0,2,1:T(8,128)(2,1)S(1)}, bf16[20,4,2,128]{3,0,2,1:T(8,128)(2,1)S(1)}, u32[]{:S(2)}, u32[]{:S(2)}) collective-permute-start(bf16[20,4,2,128]{3,0,2,1:T(8,128)(2,1)S(1)} %get-tuple-element.7), channel_id=1, source_target_pairs={{0,1},{1,2},{2,3},{3,4},{4,5},{5,6},{6,7},{7,8},{8,9},{9,10},{10,1... | collective-permute-start | bytes 122888 | tf_op jit(solution)/shard_map/ppermute | solution.py:24

commit v3 on v2

--- a/solution.py
+++ b/solution.py
@@ -18,11 +18,11 @@
 
 def halos(x):
     wide_x, wide_y = x.shape[1], x.shape[2]
-    low = x.astype(jnp.bfloat16)
-    x_before = lax.ppermute(low[:, wide_x - 2 :], "gx", ring("gx", 1))
-    x_after = lax.ppermute(low[:, :2], "gx", ring("gx", -1))
-    y_before = lax.ppermute(low[:, :, wide_y - 2 :], "gy", ring("gy", 1))
-    y_after = lax.ppermute(low[:, :, :2], "gy", ring("gy", -1))
+    low = jnp.bfloat16
+    x_before = lax.ppermute(x[:, wide_x - 2 :].astype(low), "gx", ring("gx", 1))
+    x_after = lax.ppermute(x[:, :2].astype(low), "gx", ring("gx", -1))
+    y_before = lax.ppermute(x[:, :, wide_y - 2 :].astype(low), "gy", ring("gy", 1))
+    y_after = lax.ppermute(x[:, :, :2].astype(low), "gy", ring("gy", -1))
     return x_before, x_after, y_before, y_after
 
 
@@ -56,8 +56,8 @@
     slope_y, curve_y = stencil(lambda k: pad_y[:, :, 2 + k : 2 + k + wide_y])
     slope_m = circulant(depth, {1: 8.0, -1: -8.0, 2: -1.0, -2: 1.0})
     curve_m = circulant(depth, {1: 16.0, -1: 16.0, 2: -1.0, -2: -1.0, 0: -30.0})
-    slope_z = jnp.einsum("fxyz,zw->fxyw", field_set, slope_m, precision=lax.Precision.HIGHEST) / 12.0
-    curve_z = jnp.einsum("fxyz,zw->fxyw", field_set, curve_m, precision=lax.Precision.HIGHEST) / 12.0
+    slope_z = jnp.einsum("fxyz,zw->fxyw", field_set, slope_m, precision=lax.Precision.HIGH) / 12.0
+    curve_z = jnp.einsum("fxyz,zw->fxyw", field_set, curve_m, precision=lax.Precision.HIGH) / 12.0
     return -(velocity_x * slope_x + velocity_y * slope_y + velocity_z * slope_z) + diffusivity[
         :, None, None, None
     ] * (curve_x + curve_y + curve_z)

time: 85.5 us -> 85 us (level)
  transfers between devices with their start and end apart: 8 -> 8, of which waited for: 1 -> 1; matrix products, arithmetic and copies ran while one was open for 24% -> 25% of each run, Pallas kernels for 0% -> 0%
where the time goes in v3:
time: 85 us; the launch traced here: 84.5 us
  starting transfers between devices  50.2 us (59%)
  matrix products  22.9 us (27%)
  waiting for transfers between devices  7.95 us (9%)
  local copies, waits for them, and re-layouts  2.89 us (3%)
    ppermute x2, starting transfers between devices, halos(): y_after = lax.ppermute(x[:, :, :2].astype(low), 'gy', ring('gy', -1))  21.9 us
    ppermute x2, starting transfers between devices, halos(): x_after = lax.ppermute(x[:, :2].astype(low), 'gx', ring('gx', -1))  20.7 us
    dot_general x1, matrix products, network(): jnp.einsum('bzh,hk->bzk', hidden, w_mid, preferred_element_type=jnp.float32)  12.1 us
    ppermute x2, waiting for transfers between devices, halos(): lax.ppermute(x[:, :, wide_y - 2:].astype(low), 'gy', ring('gy', 1))  7.94 us
    dot_general x1, matrix products, network(): jnp.einsum('bzj,fj->bfz', hidden, w_out, preferred_element_type=jnp.float32)  7.1 us
    ppermute x2, starting transfers between devices, halos(): lax.ppermute(x[:, :, wide_y - 2:].astype(low), 'gy', ring('gy', 1))  3.84 us
    ppermute x2, starting transfers between devices, halos(): x_before = lax.ppermute(x[:, wide_x - 2:].astype(low), 'gx', ring('gx', 1))  3.84 us
  transfers between devices with their start and end apart: 8, of which 1 were waited for; matrix products, arithmetic and copies ran while one was open for 25% of the time, Pallas kernels for 0%

profile of v3, /device:TPU:8, one launch (start us, length us, event | category | flops | bytes accessed | tf_op | source)
XLA Modules:
  0.0 84.5 jit_solution(2739177027355336416)
XLA Ops:
  0.0 0.0 copy-start
  0.0 1.1 %copy.52 = bf16[20,4,6,128]{3,0,2,1:T(8,128)(2,1)S(1)} copy(f32[20,4,6,128]{3,1,2,0:T(4,128)} %param.11) | data formatting | bytes 368640 | tf_op args[0]
  1.2 14.3 %collective-permute-start.2 = (bf16[20,4,2,128]{3,0,2,1:T(8,128)(2,1)S(1)}, bf16[20,4,2,128]{3,0,2,1:T(8,128)(2,1)S(1)}, u32[]{:S(2)}, u32[]{:S(2)}) collective-permute-start(bf16[20,4,2,128]{3,0,2,1:T(8,128)(2,1)S(1)} %get-tuple-element.12), channel_id=1, source_target_pairs={{0,31},{1,0},{2,1},{3,2},{4,3},{5,4},{6,5},{7,6},{8,7},{9,8},{10,9... | collective-permute-start | bytes 122888 | tf_op jit(solution)/shard_map/ppermute | solution.py:25
  15.5 1.9 %collective-permute-start.3 = (bf16[20,4,2,128]{3,0,2,1:T(8,128)(2,1)S(1)}, bf16[20,4,2,128]{3,0,2,1:T(8,128)(2,1)S(1)}, u32[]{:S(2)}, u32[]{:S(2)}) collective-permute-start(bf16[20,4,2,128]{3,0,2,1:T(8,128)(2,1)S(1)} %get-tuple-element.11), channel_id=1, source_target_pairs={{0,1},{1,2},{2,3},{3,4},{4,5},{5,6},{6,7},{7,8},{8,9},{9,10},{10,1... | collective-permute-start | bytes 122888 | tf_op jit(solution)/shard_map/ppermute | solution.py:24
  17.5 11.0 %collective-permute-start = (bf16[20,2,6,128]{3,0,2,1:T(8,128)(2,1)S(1)}, bf16[20,2,6,128]{3,0,2,1:T(8,128)(2,1)S(1)}, u32[]{:S(2)}, u32[]{:S(2)}) collective-permute-start(bf16[20,2,6,128]{3,0,2,1:T(8,128)(2,1)S(1)} %get-tuple-element.10), channel_id=1, source_target_pairs={{0,992},{32,0},{64,32},{96,64},{128,96},{160,128},{192,160},{224,1... | collective-permute-start | bytes 184328 | tf_op jit(solution)/shard_map/ppermute | solution.py:23
  28.5 1.9 %collective-permute-start.1 = (bf16[20,2,6,128]{3,0,2,1:T(8,128)(2,1)S(1)}, bf16[20,2,6,128]{3,0,2,1:T(8,128)(2,1)S(1)}, u32[]{:S(2)}, u32[]{:S(2)}) collective-permute-start(bf16[20,2,6,128]{3,0,2,1:T(8,128)(2,1)S(1)} %get-tuple-element.9), channel_id=1, source_target_pairs={{0,32},{32,64},{64,96},{96,128},{128,160},{160,192},{192,224},{224... | collective-permute-start | bytes 184328 | tf_op jit(solution)/shard_map/ppermute | solution.py:22
  30.4 0.8 broadcast_in_dim.20
  31.1 0.1 select_reduce_fusion
  31.3 0.3 fusion.37
  31.6 0.0 copy-done
  31.6 0.0 copy-start.2
  31.6 12.1 %fusion = f32[18,128,800]{1,2,0:T(8,128)} fusion(bf16[1600,800]{0,1:T(8,128)(2,1)S(1)} %copy-done, bf16[18,20,128]{2,0,1:T(8,128)(2,1)S(1)} %fusion.37, bf16[20,1600]{1,0:T(8,128)(2,1)} %param.13), kind=kOutput, calls=%fused_computation.2 | convolution fusion | flops 6064128000 | bytes 10088960 | tf_op jit(solution)/shard_map/bzh,hk->bzk/dot_general | solution.py:71
  43.7 0.0 copy-done.2
  43.7 0.0 copy-start.3
  43.7 0.0 copy-start.1
  43.7 7.1 %fusion.5 = bf16[18,128,20]{1,2,0:T(8,128)(2,1)S(1)} fusion(f32[18,128,800]{1,2,0:T(8,128)} %fusion, bf16[800,400]{0,1:T(8,128)(2,1)} %param.15, bf16[20,400]{1,0:T(8,128)(2,1)S(1)} %copy-done.2), kind=kOutput, calls=%fused_computation.7 | convolution fusion | flops 1525248000 | bytes 8120960 | tf_op jit(solution)/shard_map/bzj,fj->bfz/dot_general | solution.py:76
  50.8 0.0 copy-start.4
  50.8 0.0 copy-start.5
  50.8 0.2 fusion.24
  51.1 0.0 copy-done.3
  51.1 0.0 copy-done.1
  51.1 0.1 copy.34
  51.2 0.1 copy.32
  51.2 0.0 collective-permute-done.2
  51.3 0.0 collective-permute-done.3
  51.3 0.0 collective-permute-done
  51.3 0.0 collective-permute-done.1
  51.3 1.2 %fusion.15 = f32[20,4,6,128]{3,0,2,1:T(8,128)S(1)} fusion(f32[128,128,1,1]{1,0,3,2:T(8,128)} %constant.52, f32[20,4,6,128]{3,0,2,1:T(8,128)S(1)} %copy.34, f32[20,4,2,128]{3,0,2,1:T(8,128)S(1)} %convert_element_type.60, f32[20,4,2,128]{3,0,2,1:T(8,128)S(1)} %convert_element_type.61, f32[20,2,6,128]{3,0,2,1:T(8,128)S(1)} %convert_element_type.58, ...), kind=kOutput, calls=%fused_computation.21 | convolution fusion | flops 48537600 | bytes 1393152 | tf_op jit(solution)/shard_map/fxyz,zw->fxyw/dot_general | solution.py:60
  52.5 1.2 %fusion.57 = (bf16[20,4,6,128]{3,0,2,1:T(8,128)(2,1)S(1)}, f32[20,4,6,128]{3,0,2,1:T(8,128)S(1)}) fusion(f32[20,4,6,128]{3,0,2,1:T(8,128)S(1)} %copy.34, f32[20,4,6,128]{3,0,2,1:T(8,128)S(1)} %bitcast.62, f32[20,4,6,128]{3,0,2,1:T(8,128)S(1)} %fusion.15, f32[128,128,1,1]{1,0,3,2:T(8,128)} %constant.51, f32[20,4,2,128]{3,0,2,1:T(8,128)S(1)} %convert_element_type.61, ...), kind=kOutput, calls=%fused_computation.90 | convolution fusion | flops 48844800 | bytes 2105344 | tf_op jit(solution)/shard_map/fxyz,zw->fxyw/dot_general | solution.py:59
  53.8 9.7 %collective-permute-start.4 = (bf16[20,2,6,128]{3,0,2,1:T(8,128)(2,1)S(1)}, bf16[20,2,6,128]{3,0,2,1:T(8,128)(2,1)S(1)}, u32[]{:S(2)}, u32[]{:S(2)}) collective-permute-start(bf16[20,2,6,128]{3,0,2,1:T(8,128)(2,1)S(1)} %get-tuple-element.6), channel_id=1, source_target_pairs={{0,992},{32,0},{64,32},{96,64},{128,96},{160,128},{192,160},{224,1... | collective-permute-start | bytes 184328 | tf_op jit(solution)/shard_map/ppermute | solution.py:23
  63.4 1.9 %collective-permute-start.5 = (bf16[20,2,6,128]{3,0,2,1:T(8,128)(2,1)S(1)}, bf16[20,2,6,128]{3,0,2,1:T(8,128)(2,1)S(1)}, u32[]{:S(2)}, u32[]{:S(2)}) collective-permute-start(bf16[20,2,6,128]{3,0,2,1:T(8,128)(2,1)S(1)} %get-tuple-element.5), channel_id=1, source_target_pairs={{0,32},{32,64},{64,96},{96,128},{128,160},{160,192},{192,224},{224... | collective-permute-start | bytes 184328 | tf_op jit(solution)/shard_map/ppermute | solution.py:22
  65.4 7.6 %collective-permute-start.6 = (bf16[20,4,2,128]{3,0,2,1:T(8,128)(2,1)S(1)}, bf16[20,4,2,128]{3,0,2,1:T(8,128)(2,1)S(1)}, u32[]{:S(2)}, u32[]{:S(2)}) collective-permute-start(bf16[20,4,2,128]{3,0,2,1:T(8,128)(2,1)S(1)} %get-tuple-element.8), channel_id=1, source_target_pairs={{0,31},{1,0},{2,1},{3,2},{4,3},{5,4},{6,5},{7,6},{8,7},{9,8},{10,9... | collective-permute-start | bytes 122888 | tf_op jit(solution)/shard_map/ppermute | solution.py:25
  73.0 1.9 %collective-permute-start.7 = (bf16[20,4,2,128]{3,0,2,1:T(8,128)(2,1)S(1)}, bf16[20,4,2,128]{3,0,2,1:T(8,128)(2,1)S(1)}, u32[]{:S(2)}, u32[]{:S(2)}) collective-permute-start(bf16[20,4,2,128]{3,0,2,1:T(8,128)(2,1)S(1)} %get-tuple-element.7), channel_id=1, source_target_pairs={{0,1},{1,2},{2,3},{3,4},{4,5},{5,6},{6,7},{7,8},{8,9},{9,10},{10,1... | collective-permute-start | bytes 122888 | tf_op jit(solution)/shard_map/ppermute | solution.py:24
  74.9 0.0 collective-permute-done.6
  74.9 7.9 %collective-permute-done.7 = bf16[20,4,2,128]{3,0,2,1:T(8,128)(2,1)S(1)} collective-permute-done((bf16[20,4,2,128]{3,0,2,1:T(8,128)(2,1)S(1)}, bf16[20,4,2,128]{3,0,2,1:T(8,128)(2,1)S(1)}, u32[]{:S(2)}, u32[]{:S(2)}) %collective-permute-start.7) | collective-permute-done | bytes 40992 | tf_op jit(solution)/shard_map/ppermute | solution.py:24
  82.9 0.0 collective-permute-done.4
  82.9 0.0 collective-permute-done.5
  82.9 0.0 copy-done.4
  82.9 0.3 fusion.6
  83.3 0.0 copy-done.5
  83.3 0.4 fusion.20
  83.7 0.8 copy.35
  (14 shorter events, 0.2 us)
Async XLA Ops:
  0.0 31.6 %copy-start = (bf16[1600,800]{0,1:T(8,128)(2,1)S(1)}, bf16[1600,800]{0,1:T(8,128)(2,1)}, u32[]{:S(2)}) copy-start(bf16[1600,800]{0,1:T(8,128)(2,1)} %param.14) | copy-start | bytes 7680004
  1.2 50.1 %collective-permute-start.2 = (bf16[20,4,2,128]{3,0,2,1:T(8,128)(2,1)S(1)}, bf16[20,4,2,128]{3,0,2,1:T(8,128)(2,1)S(1)}, u32[]{:S(2)}, u32[]{:S(2)}) collective-permute-start(bf16[20,4,2,128]{3,0,2,1:T(8,128)(2,1)S(1)} %get-tuple-element.12), channel_id=1, source_target_pairs={{0,31},{1,0},{2,1},{3,2},{4,3},{5,4},{6,5},{7,6},{8,7},{9,8},{10,9... | collective-permute-start | bytes 122888 | tf_op jit(solution)/shard_map/ppermute | solution.py:25
  15.5 35.8 %collective-permute-start.3 = (bf16[20,4,2,128]{3,0,2,1:T(8,128)(2,1)S(1)}, bf16[20,4,2,128]{3,0,2,1:T(8,128)(2,1)S(1)}, u32[]{:S(2)}, u32[]{:S(2)}) collective-permute-start(bf16[20,4,2,128]{3,0,2,1:T(8,128)(2,1)S(1)} %get-tuple-element.11), channel_id=1, source_target_pairs={{0,1},{1,2},{2,3},{3,4},{4,5},{5,6},{6,7},{7,8},{8,9},{9,10},{10,1... | collective-permute-start | bytes 122888 | tf_op jit(solution)/shard_map/ppermute | solution.py:24
  17.5 33.8 %collective-permute-start = (bf16[20,2,6,128]{3,0,2,1:T(8,128)(2,1)S(1)}, bf16[20,2,6,128]{3,0,2,1:T(8,128)(2,1)S(1)}, u32[]{:S(2)}, u32[]{:S(2)}) collective-permute-start(bf16[20,2,6,128]{3,0,2,1:T(8,128)(2,1)S(1)} %get-tuple-element.10), channel_id=1, source_target_pairs={{0,992},{32,0},{64,32},{96,64},{128,96},{160,128},{192,160},{224,1... | collective-permute-start | bytes 184328 | tf_op jit(solution)/shard_map/ppermute | solution.py:23
  28.5 22.9 %collective-permute-start.1 = (bf16[20,2,6,128]{3,0,2,1:T(8,128)(2,1)S(1)}, bf16[20,2,6,128]{3,0,2,1:T(8,128)(2,1)S(1)}, u32[]{:S(2)}, u32[]{:S(2)}) collective-permute-start(bf16[20,2,6,128]{3,0,2,1:T(8,128)(2,1)S(1)} %get-tuple-element.9), channel_id=1, source_target_pairs={{0,32},{32,64},{64,96},{96,128},{128,160},{160,192},{192,224},{224... | collective-permute-start | bytes 184328 | tf_op jit(solution)/shard_map/ppermute | solution.py:22
  31.6 12.1 %copy-start.2 = (bf16[20,400]{1,0:T(8,128)(2,1)S(1)}, bf16[20,400]{1,0:T(8,128)(2,1)}, u32[]{:S(2)}) copy-start(bf16[20,400]{1,0:T(8,128)(2,1)} %param.16) | copy-start | bytes 48004
  43.7 7.4 %copy-start.3 = (f32[20]{0:T(128)S(1)}, f32[20]{0:T(128)}, u32[]{:S(2)}) copy-start(f32[20]{0:T(128)} %param.17) | copy-start | bytes 244
  43.7 7.4 %copy-start.1 = (f32[20,4,6,128]{3,1,2,0:T(4,128)S(1)}, f32[20,4,6,128]{3,1,2,0:T(4,128)}, u32[]{:S(2)}) copy-start(f32[20,4,6,128]{3,1,2,0:T(4,128)} %param.11) | copy-start | bytes 737284
  50.8 32.1 %copy-start.4 = (f32[128,128,1,1]{1,0,3,2:T(8,128)S(1)}, f32[128,128,1,1]{1,0,3,2:T(8,128)}, u32[]{:S(2)}) copy-start(f32[128,128,1,1]{1,0,3,2:T(8,128)} %constant.52) | copy-start | bytes 196612
  50.8 32.4 %copy-start.5 = (f32[128,128,1,1]{1,0,3,2:T(8,128)S(1)}, f32[128,128,1,1]{1,0,3,2:T(8,128)}, u32[]{:S(2)}) copy-start(f32[128,128,1,1]{1,0,3,2:T(8,128)} %constant.51) | copy-start | bytes 196612
  53.8 29.1 %collective-permute-start.4 = (bf16[20,2,6,128]{3,0,2,1:T(8,128)(2,1)S(1)}, bf16[20,2,6,128]{3,0,2,1:T(8,128)(2,1)S(1)}, u32[]{:S(2)}, u32[]{:S(2)}) collective-permute-start(bf16[20,2,6,128]{3,0,2,1:T(8,128)(2,1)S(1)} %get-tuple-element.6), channel_id=1, source_target_pairs={{0,992},{32,0},{64,32},{96,64},{128,96},{160,128},{192,160},{224,1... | collective-permute-start | bytes 184328 | tf_op jit(solution)/shard_map/ppermute | solution.py:23
  63.4 19.4 %collective-permute-start.5 = (bf16[20,2,6,128]{3,0,2,1:T(8,128)(2,1)S(1)}, bf16[20,2,6,128]{3,0,2,1:T(8,128)(2,1)S(1)}, u32[]{:S(2)}, u32[]{:S(2)}) collective-permute-start(bf16[20,2,6,128]{3,0,2,1:T(8,128)(2,1)S(1)} %get-tuple-element.5), channel_id=1, source_target_pairs={{0,32},{32,64},{64,96},{96,128},{128,160},{160,192},{192,224},{224... | collective-permute-start | bytes 184328 | tf_op jit(solution)/shard_map/ppermute | solution.py:22
  65.4 9.5 %collective-permute-start.6 = (bf16[20,4,2,128]{3,0,2,1:T(8,128)(2,1)S(1)}, bf16[20,4,2,128]{3,0,2,1:T(8,128)(2,1)S(1)}, u32[]{:S(2)}, u32[]{:S(2)}) collective-permute-start(bf16[20,4,2,128]{3,0,2,1:T(8,128)(2,1)S(1)} %get-tuple-element.8), channel_id=1, source_target_pairs={{0,31},{1,0},{2,1},{3,2},{4,3},{5,4},{6,5},{7,6},{8,7},{9,8},{10,9... | collective-permute-start | bytes 122888 | tf_op jit(solution)/shard_map/ppermute | solution.py:25
  73.0 9.9 %collective-permute-start.7 = (bf16[20,4,2,128]{3,0,2,1:T(8,128)(2,1)S(1)}, bf16[20,4,2,128]{3,0,2,1:T(8,128)(2,1)S(1)}, u32[]{:S(2)}, u32[]{:S(2)}) collective-permute-start(bf16[20,4,2,128]{3,0,2,1:T(8,128)(2,1)S(1)} %get-tuple-element.7), channel_id=1, source_target_pairs={{0,1},{1,2},{2,3},{3,4},{4,5},{5,6},{6,7},{7,8},{8,9},{9,10},{10,1... | collective-permute-start | bytes 122888 | tf_op jit(solution)/shard_map/ppermute | solution.py:24

commit v4 on v3

--- a/solution.py
+++ b/solution.py
@@ -16,13 +16,29 @@
     return [(i, (i + step) % peers) for i in range(peers)]
 
 
+def swap_faces(first, last, axis):
+    peers = lax.axis_size(axis)
+    if peers % 2:
+        before = lax.ppermute(last, axis, ring(axis, 1))
+        after = lax.ppermute(first, axis, ring(axis, -1))
+        return before, after
+    even = lax.axis_index(axis) % 2 == 0
+    outer = [(i, (i + 1) % peers) for i in range(1, peers, 2)]
+    outer = outer + [(j, i) for i, j in outer]
+    inner = [(i, i + 1) for i in range(0, peers, 2)]
+    inner = inner + [(j, i) for i, j in inner]
+    got_outer = lax.ppermute(jnp.where(even, first, last), axis, outer)
+    got_inner = lax.ppermute(jnp.where(even, last, first), axis, inner)
+    before = jnp.where(even, got_outer, got_inner)
+    after = jnp.where(even, got_inner, got_outer)
+    return before, after
+
+
 def halos(x):
     wide_x, wide_y = x.shape[1], x.shape[2]
     low = jnp.bfloat16
-    x_before = lax.ppermute(x[:, wide_x - 2 :].astype(low), "gx", ring("gx", 1))
-    x_after = lax.ppermute(x[:, :2].astype(low), "gx", ring("gx", -1))
-    y_before = lax.ppermute(x[:, :, wide_y - 2 :].astype(low), "gy", ring("gy", 1))
-    y_after = lax.ppermute(x[:, :, :2].astype(low), "gy", ring("gy", -1))
+    x_before, x_after = swap_faces(x[:, :2].astype(low), x[:, wide_x - 2 :].astype(low), "gx")
+    y_before, y_after = swap_faces(x[:, :, :2].astype(low), x[:, :, wide_y - 2 :].astype(low), "gy")
     return x_before, x_after, y_before, y_after
 
 
@@ -56,8 +72,14 @@
     slope_y, curve_y = stencil(lambda k: pad_y[:, :, 2 + k : 2 + k + wide_y])
     slope_m = circulant(depth, {1: 8.0, -1: -8.0, 2: -1.0, -2: 1.0})
     curve_m = circulant(depth, {1: 16.0, -1: 16.0, 2: -1.0, -2: -1.0, 0: -30.0})
-    slope_z = jnp.einsum("fxyz,zw->fxyw", field_set, slope_m, precision=lax.Precision.HIGH) / 12.0
-    curve_z = jnp.einsum("fxyz,zw->fxyw", field_set, curve_m, precision=lax.Precision.HIGH) / 12.0
+    both = jnp.einsum(
+        "fxyz,zw->fxyw",
+        field_set,
+        jnp.concatenate([slope_m, curve_m], axis=1),
+        precision=lax.Precision.HIGH,
+    )
+    slope_z = both[..., :depth] / 12.0
+    curve_z = both[..., depth:] / 12.0
     return -(velocity_x * slope_x + velocity_y * slope_y + velocity_z * slope_z) + diffusivity[
         :, None, None, None
     ] * (curve_x + curve_y + curve_z)
@@ -84,19 +106,18 @@
     share = 3 * blocks // 8
     spread = min(share, blocks - share)
     cap = min(blocks, share + spread)
-    live_mask = reacting.reshape(blocks)
-    order = jnp.arange(blocks)
-    local_rank = jnp.sum(jnp.where(order[None, :] < order[:, None], live_mask[None, :], 0), axis=1)
+    live = reacting == 1
+    flat = jnp.arange(blocks).reshape(wide_x, wide_y)
+    earlier = flat[None, None, :, :] < flat[:, :, None, None]
+    local_rank = jnp.sum(jnp.where(earlier & live[None, None, :, :], 1, 0), axis=(2, 3))
     keep_pick = (
-        (local_rank[None, :] == jnp.arange(cap)[:, None]) & (live_mask[None, :] == 1)
+        (local_rank[None, :, :] == jnp.arange(cap)[:, None, None]) & live[None, :, :]
     ).astype(jnp.bfloat16)
-    rows = jnp.moveaxis(flow_state.reshape(fields, blocks, depth_z), 1, 0).astype(jnp.bfloat16)
-    batch = jnp.einsum("qb,bfz->qfz", keep_pick, rows, preferred_element_type=jnp.float32).astype(
-        jnp.bfloat16
-    )
+    batch = jnp.einsum(
+        "qxy,fxyz->qfz", keep_pick, flow_state.astype(jnp.bfloat16), preferred_element_type=jnp.float32
+    ).astype(jnp.bfloat16)
     results = network(batch, w_in, w_mid, w_low, w_out)
-    source = jnp.einsum("qb,qfz->bfz", keep_pick, results, preferred_element_type=jnp.float32)
-    reaction = jnp.moveaxis(source, 0, 1).reshape(fields, wide_x, wide_y, depth_z)
+    reaction = jnp.einsum("qxy,qfz->fxyz", keep_pick, results, preferred_element_type=jnp.float32)
 
     def tendency(field_set):
         return transport(field_set, diffusivity) + reaction_gain * reaction

time: 85 us -> 72.7 us (0.86)
  the two profiles are of different devices: /device:TPU:8 before, /device:TPU:64 now
where the time goes in v4:
time: 72.7 us; the launch traced here: 72.3 us
  starting transfers between devices  38.7 us (53%)
  matrix products  20.4 us (28%)
  waiting for transfers between devices  7.98 us (11%)
  other arithmetic  2.99 us (4%)
  local copies, waits for them, and re-layouts  2 us (3%)
    ppermute x4, starting transfers between devices, swap_faces(): got_outer = lax.ppermute(jnp.where(even, first, last), axis, outer)  27.7 us
    dot_general x1, matrix products, network(): jnp.einsum('bzh,hk->bzk', hidden, w_mid, preferred_element_type=jnp.float32)  12.1 us
    ppermute x4, starting transfers between devices, swap_faces(): got_inner = lax.ppermute(jnp.where(even, last, first), axis, inner)  10.9 us
    dot_general x1, matrix products, network(): jnp.einsum('bzj,fj->bfz', hidden, w_out, preferred_element_type=jnp.float32)  6.99 us
    ppermute x4, waiting for transfers between devices, swap_faces(): got_outer = lax.ppermute(jnp.where(even, first, last), axis, outer)  5.16 us
    ppermute x4, waiting for transfers between devices, swap_faces(): got_inner = lax.ppermute(jnp.where(even, last, first), axis, inner)  2.82 us
  transfers between devices with their start and end apart: 8, of which 2 were waited for; matrix products, arithmetic and copies ran while one was open for 30% of the time, Pallas kernels for 0%

profile of v4, /device:TPU:64, one launch (start us, length us, event | category | flops | bytes accessed | tf_op | source)
XLA Modules:
  0.0 72.3 jit_solution(6466369487863976830)
XLA Ops:
  0.0 0.0 copy-start
  0.0 1.1 %copy.57 = bf16[20,4,6,128]{3,0,2,1:T(8,128)(2,1)S(1)} copy(f32[20,4,6,128]{3,1,2,0:T(4,128)} %param.11) | data formatting | bytes 368640 | tf_op args[0]
  1.2 0.6 broadcast_select_fusion.7
  1.8 5.2 %collective-permute-start.2 = (bf16[20,4,2,128]{3,0,2,1:T(8,128)(2,1)}, bf16[20,4,2,128]{3,0,2,1:T(8,128)(2,1)S(1)}, u32[]{:S(2)}, u32[]{:S(2)}) collective-permute-start(bf16[20,4,2,128]{3,0,2,1:T(8,128)(2,1)} %get-tuple-element.17), channel_id=1, source_target_pairs={{0,1},{2,3},{4,5},{6,7},{8,9},{10,11},{12,13},{14,15},{16,17},{18,... | collective-permute-start | bytes 122888 | tf_op jit(solution)/shard_map/ppermute | solution.py:31
  7.0 7.1 %collective-permute-start.3 = (bf16[20,4,2,128]{3,0,2,1:T(8,128)(2,1)}, bf16[20,4,2,128]{3,0,2,1:T(8,128)(2,1)S(1)}, u32[]{:S(2)}, u32[]{:S(2)}) collective-permute-start(bf16[20,4,2,128]{3,0,2,1:T(8,128)(2,1)} %get-tuple-element.18), channel_id=1, source_target_pairs={{1,2},{3,4},{5,6},{7,8},{9,10},{11,12},{13,14},{15,16},{17,18},{19... | collective-permute-start | bytes 122888 | tf_op jit(solution)/shard_map/ppermute | solution.py:30
  14.2 1.9 %collective-permute-start = (bf16[20,2,6,128]{3,0,2,1:T(8,128)(2,1)S(1)}, bf16[20,2,6,128]{3,0,2,1:T(8,128)(2,1)S(1)}, u32[]{:S(2)}, u32[]{:S(2)}) collective-permute-start(bf16[20,2,6,128]{3,0,2,1:T(8,128)(2,1)S(1)} %get-tuple-element.15), channel_id=1, source_target_pairs={{0,32},{64,96},{128,160},{192,224},{256,288},{320,352},{384,416},{... | collective-permute-start | bytes 184328 | tf_op jit(solution)/shard_map/ppermute | solution.py:31
  16.1 14.3 %collective-permute-start.1 = (bf16[20,2,6,128]{3,0,2,1:T(8,128)(2,1)S(1)}, bf16[20,2,6,128]{3,0,2,1:T(8,128)(2,1)S(1)}, u32[]{:S(2)}, u32[]{:S(2)}) collective-permute-start(bf16[20,2,6,128]{3,0,2,1:T(8,128)(2,1)S(1)} %get-tuple-element.16), channel_id=1, source_target_pairs={{32,64},{96,128},{160,192},{224,256},{288,320},{352,384},{416,448}... | collective-permute-start | bytes 184328 | tf_op jit(solution)/shard_map/ppermute | solution.py:30
  30.4 0.7 broadcast_compare_fusion
  31.1 0.6 select_reduce_fusion
  31.7 0.3 fusion.32
  32.0 0.0 copy-done
  32.0 12.1 %fusion = f32[18,128,800]{1,2,0:T(8,128)} fusion(bf16[1600,800]{0,1:T(8,128)(2,1)S(1)} %copy-done, bf16[18,20,128,1]{2,0,3,1:T(8,128)(2,1)S(1)} %fusion.32, bf16[20,1600]{1,0:T(8,128)(2,1)} %param.13), kind=kOutput, calls=%fused_computation.2 | convolution fusion | flops 6064128000 | bytes 10088960 | tf_op jit(solution)/shard_map/bzh,hk->bzk/dot_general | solution.py:93
  44.1 0.0 copy-start.1
  44.1 0.0 copy-start.2
  44.1 0.0 copy-start.3
  44.1 7.0 %fusion.5 = bf16[18,128,20]{1,2,0:T(8,128)(2,1)S(1)} fusion(f32[18,128,800]{1,2,0:T(8,128)} %fusion, bf16[800,400]{0,1:T(8,128)(2,1)} %param.15, bf16[20,400]{1,0:T(8,128)(2,1)} %param.16), kind=kOutput, calls=%fused_computation.7 | convolution fusion | flops 1525248000 | bytes 8120960 | tf_op jit(solution)/shard_map/bzj,fj->bfz/dot_general | solution.py:98
  51.1 0.2 fusion.35
  51.3 0.0 copy-done.1
  51.3 0.0 copy-done.2
  51.4 0.4 convolution_bitcast_fusion
  51.8 0.0 copy-done.3
  51.8 0.1 copy.32
  51.8 0.0 collective-permute-done.2
  51.8 0.0 collective-permute-done.3
  51.9 0.0 collective-permute-done
  51.9 0.0 collective-permute-done.1
  51.9 0.4 fusion.52
  52.4 0.4 fusion.54
  52.8 4.4 %collective-permute-start.7 = (bf16[20,4,2,128]{3,0,2,1:T(8,128)(2,1)S(1)}, bf16[20,4,2,128]{3,0,2,1:T(8,128)(2,1)S(1)}, u32[]{:S(2)}, u32[]{:S(2)}) collective-permute-start(bf16[20,4,2,128]{3,0,2,1:T(8,128)(2,1)S(1)} %get-tuple-element.11), channel_id=1, source_target_pairs={{1,2},{3,4},{5,6},{7,8},{9,10},{11,12},{13,14},{15,16},{17,18},{19... | collective-permute-start | bytes 122888 | tf_op jit(solution)/shard_map/ppermute | solution.py:30
  57.2 1.9 %collective-permute-start.6 = (bf16[20,4,2,128]{3,0,2,1:T(8,128)(2,1)S(1)}, bf16[20,4,2,128]{3,0,2,1:T(8,128)(2,1)S(1)}, u32[]{:S(2)}, u32[]{:S(2)}) collective-permute-start(bf16[20,4,2,128]{3,0,2,1:T(8,128)(2,1)S(1)} %get-tuple-element.12), channel_id=1, source_target_pairs={{0,1},{2,3},{4,5},{6,7},{8,9},{10,11},{12,13},{14,15},{16,17},{18,... | collective-permute-start | bytes 122888 | tf_op jit(solution)/shard_map/ppermute | solution.py:31
  59.2 1.9 %collective-permute-start.5 = (bf16[20,2,6,128]{3,0,2,1:T(8,128)(2,1)S(1)}, bf16[20,2,6,128]{3,0,2,1:T(8,128)(2,1)S(1)}, u32[]{:S(2)}, u32[]{:S(2)}) collective-permute-start(bf16[20,2,6,128]{3,0,2,1:T(8,128)(2,1)S(1)} %get-tuple-element.9), channel_id=1, source_target_pairs={{32,64},{96,128},{160,192},{224,256},{288,320},{352,384},{416,448}... | collective-permute-start | bytes 184328 | tf_op jit(solution)/shard_map/ppermute | solution.py:30
  61.1 1.9 %collective-permute-start.4 = (bf16[20,2,6,128]{3,0,2,1:T(8,128)(2,1)S(1)}, bf16[20,2,6,128]{3,0,2,1:T(8,128)(2,1)S(1)}, u32[]{:S(2)}, u32[]{:S(2)}) collective-permute-start(bf16[20,2,6,128]{3,0,2,1:T(8,128)(2,1)S(1)} %get-tuple-element.10), channel_id=1, source_target_pairs={{0,32},{64,96},{128,160},{192,224},{256,288},{320,352},{384,416},{... | collective-permute-start | bytes 184328 | tf_op jit(solution)/shard_map/ppermute | solution.py:31
  63.0 0.0 collective-permute-done.7
  63.0 2.8 %collective-permute-done.6 = bf16[20,4,2,128]{3,0,2,1:T(8,128)(2,1)S(1)} collective-permute-done((bf16[20,4,2,128]{3,0,2,1:T(8,128)(2,1)S(1)}, bf16[20,4,2,128]{3,0,2,1:T(8,128)(2,1)S(1)}, u32[]{:S(2)}, u32[]{:S(2)}) %collective-permute-start.6) | collective-permute-done | bytes 40992 | tf_op jit(solution)/shard_map/ppermute | solution.py:31
  65.9 5.2 %collective-permute-done.5 = bf16[20,2,6,128]{3,0,2,1:T(8,128)(2,1)S(1)} collective-permute-done((bf16[20,2,6,128]{3,0,2,1:T(8,128)(2,1)S(1)}, bf16[20,2,6,128]{3,0,2,1:T(8,128)(2,1)S(1)}, u32[]{:S(2)}, u32[]{:S(2)}) %collective-permute-start.5) | collective-permute-done | bytes 61472 | tf_op jit(solution)/shard_map/ppermute | solution.py:30
  71.0 0.0 collective-permute-done.4
  71.1 0.5 fusion.22
  71.5 0.8 %copy.33 = f32[20,4,6,128]{3,1,2,0:T(4,128)} copy(f32[20,4,6,128]{3,0,2,1:T(8,128)S(1)} %fusion.22) | data formatting | bytes 491520 | tf_op jit(solution)/shard_map/add | solution.py:126
  (9 shorter events, 0.1 us)
Async XLA Ops:
  0.0 32.0 %copy-start = (bf16[1600,800]{0,1:T(8,128)(2,1)S(1)}, bf16[1600,800]{0,1:T(8,128)(2,1)}, u32[]{:S(2)}) copy-start(bf16[1600,800]{0,1:T(8,128)(2,1)} %param.14) | copy-start | bytes 7680004
  1.8 50.0 %collective-permute-start.2 = (bf16[20,4,2,128]{3,0,2,1:T(8,128)(2,1)}, bf16[20,4,2,128]{3,0,2,1:T(8,128)(2,1)S(1)}, u32[]{:S(2)}, u32[]{:S(2)}) collective-permute-start(bf16[20,4,2,128]{3,0,2,1:T(8,128)(2,1)} %get-tuple-element.17), channel_id=1, source_target_pairs={{0,1},{2,3},{4,5},{6,7},{8,9},{10,11},{12,13},{14,15},{16,17},{18,... | collective-permute-start | bytes 122888 | tf_op jit(solution)/shard_map/ppermute | solution.py:31
  7.0 44.9 %collective-permute-start.3 = (bf16[20,4,2,128]{3,0,2,1:T(8,128)(2,1)}, bf16[20,4,2,128]{3,0,2,1:T(8,128)(2,1)S(1)}, u32[]{:S(2)}, u32[]{:S(2)}) collective-permute-start(bf16[20,4,2,128]{3,0,2,1:T(8,128)(2,1)} %get-tuple-element.18), channel_id=1, source_target_pairs={{1,2},{3,4},{5,6},{7,8},{9,10},{11,12},{13,14},{15,16},{17,18},{19... | collective-permute-start | bytes 122888 | tf_op jit(solution)/shard_map/ppermute | solution.py:30
  14.2 37.7 %collective-permute-start = (bf16[20,2,6,128]{3,0,2,1:T(8,128)(2,1)S(1)}, bf16[20,2,6,128]{3,0,2,1:T(8,128)(2,1)S(1)}, u32[]{:S(2)}, u32[]{:S(2)}) collective-permute-start(bf16[20,2,6,128]{3,0,2,1:T(8,128)(2,1)S(1)} %get-tuple-element.15), channel_id=1, source_target_pairs={{0,32},{64,96},{128,160},{192,224},{256,288},{320,352},{384,416},{... | collective-permute-start | bytes 184328 | tf_op jit(solution)/shard_map/ppermute | solution.py:31
  16.1 35.8 %collective-permute-start.1 = (bf16[20,2,6,128]{3,0,2,1:T(8,128)(2,1)S(1)}, bf16[20,2,6,128]{3,0,2,1:T(8,128)(2,1)S(1)}, u32[]{:S(2)}, u32[]{:S(2)}) collective-permute-start(bf16[20,2,6,128]{3,0,2,1:T(8,128)(2,1)S(1)} %get-tuple-element.16), channel_id=1, source_target_pairs={{32,64},{96,128},{160,192},{224,256},{288,320},{352,384},{416,448}... | collective-permute-start | bytes 184328 | tf_op jit(solution)/shard_map/ppermute | solution.py:30
  44.1 7.2 %copy-start.1 = (f32[20,4,6,128]{3,1,2,0:T(4,128)S(1)}, f32[20,4,6,128]{3,1,2,0:T(4,128)}, u32[]{:S(2)}) copy-start(f32[20,4,6,128]{3,1,2,0:T(4,128)} %param.11) | copy-start | bytes 737284
  44.1 7.2 %copy-start.2 = (f32[128,256,1,1]{1,0,3,2:T(8,128)S(1)}, f32[128,256,1,1]{1,0,3,2:T(8,128)}, u32[]{:S(2)}) copy-start(f32[128,256,1,1]{1,0,3,2:T(8,128)} %constant.82) | copy-start | bytes 393220
  44.1 7.7 %copy-start.3 = (f32[20]{0:T(128)S(1)}, f32[20]{0:T(128)}, u32[]{:S(2)}) copy-start(f32[20]{0:T(128)} %param.17) | copy-start | bytes 244
  52.8 10.2 %collective-permute-start.7 = (bf16[20,4,2,128]{3,0,2,1:T(8,128)(2,1)S(1)}, bf16[20,4,2,128]{3,0,2,1:T(8,128)(2,1)S(1)}, u32[]{:S(2)}, u32[]{:S(2)}) collective-permute-start(bf16[20,4,2,128]{3,0,2,1:T(8,128)(2,1)S(1)} %get-tuple-element.11), channel_id=1, source_target_pairs={{1,2},{3,4},{5,6},{7,8},{9,10},{11,12},{13,14},{15,16},{17,18},{19... | collective-permute-start | bytes 122888 | tf_op jit(solution)/shard_map/ppermute | solution.py:30
  57.2 8.6 %collective-permute-start.6 = (bf16[20,4,2,128]{3,0,2,1:T(8,128)(2,1)S(1)}, bf16[20,4,2,128]{3,0,2,1:T(8,128)(2,1)S(1)}, u32[]{:S(2)}, u32[]{:S(2)}) collective-permute-start(bf16[20,4,2,128]{3,0,2,1:T(8,128)(2,1)S(1)} %get-tuple-element.12), channel_id=1, source_target_pairs={{0,1},{2,3},{4,5},{6,7},{8,9},{10,11},{12,13},{14,15},{16,17},{18,... | collective-permute-start | bytes 122888 | tf_op jit(solution)/shard_map/ppermute | solution.py:31
  59.2 11.9 %collective-permute-start.5 = (bf16[20,2,6,128]{3,0,2,1:T(8,128)(2,1)S(1)}, bf16[20,2,6,128]{3,0,2,1:T(8,128)(2,1)S(1)}, u32[]{:S(2)}, u32[]{:S(2)}) collective-permute-start(bf16[20,2,6,128]{3,0,2,1:T(8,128)(2,1)S(1)} %get-tuple-element.9), channel_id=1, source_target_pairs={{32,64},{96,128},{160,192},{224,256},{288,320},{352,384},{416,448}... | collective-permute-start | bytes 184328 | tf_op jit(solution)/shard_map/ppermute | solution.py:30
  61.1 9.9 %collective-permute-start.4 = (bf16[20,2,6,128]{3,0,2,1:T(8,128)(2,1)S(1)}, bf16[20,2,6,128]{3,0,2,1:T(8,128)(2,1)S(1)}, u32[]{:S(2)}, u32[]{:S(2)}) collective-permute-start(bf16[20,2,6,128]{3,0,2,1:T(8,128)(2,1)S(1)} %get-tuple-element.10), channel_id=1, source_target_pairs={{0,32},{64,96},{128,160},{192,224},{256,288},{320,352},{384,416},{... | collective-permute-start | bytes 184328 | tf_op jit(solution)/shard_map/ppermute | solution.py:31
